TPU v7x, 256 devices: a whole 4x4x8 slice. The times are simulated.
256 devices in a mesh: ctx: 4 (over x_hi, core), exp: 64 (over y, z, x_lo).
Axes of the slice: x: 4 (x_hi: 2, x_lo: 2; x = x_hi * 2 + x_lo), y: 4, z: 8, core: 2. Of those that a mesh axis runs over, the one named last changes fastest.
Arguments:
- queries: bfloat16 [64, 1024, 2048], P('exp', 'ctx'), may hold values from -5 to 5
- key_rows: bfloat16 [64, 1024, 2048], P('exp', 'ctx'), may hold values from -5 to 5
- value_rows: bfloat16 [64, 1024, 2048], P('exp', 'ctx'), may hold values from -6 to 6
- residual_in: bfloat16 [64, 1024, 2048], P('exp', 'ctx'), may hold values from -6 to 6
- norm_gain: float32 [2048], replicated, may hold values from 0.1 to 1.9
- routes: int32 [64, 1024, 2], P('exp', 'ctx'), may hold values from 0 to 63, all different within a row; in each aligned block of 256 rows (0 to 255, 256 to 511, ..., all dimensions but the last counted through in order) at most 10 rows name the same one
- gate_weights: float32 [64, 1024, 2], P('exp', 'ctx'), may hold values from 0.25 to 1
- gate_up_weight: bfloat16 [64, 2048, 2, 1024], P('exp', None, None, 'ctx'), may hold values from -0.125 to 0.125
- down_weight: bfloat16 [64, 1024, 2048], P('exp', 'ctx'), may hold values from -0.1875 to 0.1875
Outputs:
- layer_out: bfloat16 [64, 1024, 2048], P('exp', 'ctx')
Inputs may be any that keep to these rules, and one draw needn't show every extreme that they name: `routes`: within the rows of one device (aligned blocks of 256 tokens in clip-then-frame order), no expert is named more than 10 times; the 2 experts of a token differ.
All inputs are finite; a program needn't handle non-finite values.
Results may differ from a plain program's by a relative error of at most 0.011.
Values may be sent and summed in bfloat16 or wider, within the bound.
No kernel may reach another device: no remote copies, remote signals or barrier semaphores. Data moves between devices by JAX's collectives and lax.ppermute only.
A program may use at most 128 MiB of HBM per device.

v0:
```python
import jax
import jax.numpy as jnp
from jax import lax
from jax.sharding import PartitionSpec as P

HEADS = 16


def far_block(block, after=None):
    if after is not None:
        block, _ = lax.optimization_barrier((block, after))
    return lax.ppermute(block, "ctx", perm=[(c, c ^ 2) for c in range(4)])


def near_blocks(block, far):
    perm = [(c, c ^ 1) for c in range(4)]
    return [block, far, lax.ppermute(block, "ctx", perm=perm), lax.ppermute(far, "ctx", perm=perm)]


def shards(
    queries,
    key_rows,
    value_rows,
    residual_in,
    norm_gain,
    routes,
    gate_weights,
    gate_up_weight,
    down_weight,
):
    clip_count, row_count, feature_count = queries.shape
    head_count = HEADS
    head_size = feature_count // head_count
    score_scale = head_size ** (-0.5)
    query_heads = queries.reshape(clip_count, row_count, head_count, head_size)
    running_max = jnp.full((clip_count, row_count, head_count), -1e30, jnp.float32)
    local_units = down_weight.shape[1]
    gate_up_local = gate_up_weight[0].reshape(feature_count, 2 * local_units)
    down_local = down_weight[0]
    key_far = far_block(key_rows)
    value_far = far_block(value_rows, key_far)
    gate_up_far = far_block(gate_up_local, value_far)
    down_far = far_block(down_local, gate_up_far)
    key_blocks = near_blocks(key_rows, key_far)
    value_blocks = near_blocks(value_rows, value_far)
    block_scores = [
        jnp.einsum(
            "cqhd,ckhd->cqhk",
            query_heads,
            block.reshape(clip_count, -1, head_count, head_size),
            preferred_element_type=jnp.float32,
        )
        * score_scale
        for block in key_blocks
    ]
    new_max = running_max
    for scores in block_scores:
        new_max = jnp.maximum(new_max, jnp.max(scores, axis=-1))
    running_sum = None
    weighted = None
    for scores, block in zip(block_scores, value_blocks):
        expo = jnp.exp(scores - new_max[..., None])
        block_sum = jnp.sum(expo, axis=-1)
        block_weighted = jnp.einsum(
            "cqhk,ckhd->cqhd",
            expo.astype(jnp.bfloat16),
            block.reshape(clip_count, -1, head_count, head_size),
            preferred_element_type=jnp.float32,
        )
        running_sum = block_sum if running_sum is None else running_sum + block_sum
        weighted = block_weighted if weighted is None else weighted + block_weighted
    final_max, final_sum = (new_max, running_sum)
    attention = (weighted / final_sum[..., None]).reshape(clip_count, row_count, feature_count)
    mixed_rows = (residual_in.astype(jnp.float32) + attention).astype(jnp.bfloat16)
    mixed_float = mixed_rows.astype(jnp.float32)
    mean_square = jnp.mean(mixed_float * mixed_float, axis=-1, keepdims=True)
    normed = (mixed_float * lax.rsqrt(mean_square + 1e-05) * norm_gain).astype(jnp.bfloat16)
    token_count = clip_count * row_count
    top_count = routes.shape[-1]
    expert_count = lax.axis_size("exp") * gate_up_weight.shape[0]
    capacity = max(2, -(-(5 * token_count * top_count) // (4 * expert_count)))
    flat_routes = routes.reshape(-1)
    one_hot = (flat_routes[:, None] == jnp.arange(expert_count, dtype=jnp.int32)[None, :]).astype(
        jnp.int32
    )
    running_count = jnp.cumsum(one_hot, axis=0)
    slot_index = jnp.sum(running_count * one_hot, axis=1) - 1
    destination = flat_routes * capacity + slot_index
    slot_token = (
        jnp.zeros((expert_count * capacity,), jnp.int32)
        .at[destination]
        .set(jnp.arange(token_count * top_count, dtype=jnp.int32) // top_count)
    )
    normed, gate_up_far = lax.optimization_barrier((normed, gate_up_far))
    send_buffer = normed.reshape(token_count, feature_count)[slot_token]
    send_buffer = send_buffer.reshape(expert_count, capacity * 8, feature_count // 8)
    gate_up_blocks = near_blocks(gate_up_local, gate_up_far)
    down_blocks = near_blocks(down_local, down_far)
    portion = lax.all_to_all(send_buffer, "exp", split_axis=0, concat_axis=0, tiled=True)
    flattened = portion.reshape(-1, feature_count)
    summed = None
    for gate_up_block, down_block in zip(gate_up_blocks, down_blocks):
        gate_and_up = jnp.dot(flattened, gate_up_block, preferred_element_type=jnp.float32)
        hidden = (
            jax.nn.silu(gate_and_up[:, :local_units]) * gate_and_up[:, local_units:]
        ).astype(jnp.bfloat16)
        group_part = jnp.dot(hidden, down_block, preferred_element_type=jnp.float32)
        group_part = group_part.astype(jnp.bfloat16).astype(jnp.float32)
        summed = group_part if summed is None else summed + group_part
    summed = summed.astype(jnp.bfloat16).reshape(portion.shape)
    returned = lax.all_to_all(summed, "exp", split_axis=0, concat_axis=0, tiled=True)
    returned = returned.reshape(-1, feature_count)
    route_slots = destination.reshape(token_count, top_count)
    route_gates = gate_weights.reshape(token_count, top_count)
    expert_sum = None
    for route in range(top_count):
        term = route_gates[:, route : route + 1] * returned[route_slots[:, route]].astype(jnp.float32)
        expert_sum = term if expert_sum is None else expert_sum + term
    layer_out = (mixed_float.reshape(token_count, feature_count) + expert_sum).astype(jnp.bfloat16)
    return layer_out.reshape(clip_count, row_count, feature_count)


def solution(mesh):
    return jax.shard_map(
        shards,
        mesh=mesh,
        in_specs=(
            P("exp", "ctx", None),
            P("exp", "ctx", None),
            P("exp", "ctx", None),
            P("exp", "ctx", None),
            P(),
            P("exp", "ctx", None),
            P("exp", "ctx", None),
            P("exp", None, None, "ctx"),
            P("exp", "ctx", None),
        ),
        out_specs=P("exp", "ctx", None),
        check_vma=False,
    )
```

profile of v0, /device:TPU:4, one launch (start us, length us, event | category | flops | bytes accessed | tf_op | source)
XLA Modules:
  0.0 299.0 jit_solution(17205131978556201615)
XLA Ops:
  16.6 12.4 %collective-permute-done = bf16[1,256,2048]{1,2,0:T(8,128)(2,1)} collective-permute-done((bf16[1,256,2048]{1,2,0:T(8,128)(2,1)}, bf16[1,256,2048]{1,2,0:T(8,128)(2,1)}, u32[]{:S(2)}, u32[]{:S(2)}) %collective-permute-start) | collective-permute-done | bytes 1048608 | tf_op jit(solution)/shard_map/ppermute | solution.py:12
  34.3 4.0 %bitcast_reduce_fusion.2 = (f32[256,16]{0,1:T(8,128)S(1)}, f32[16,256,256]{2,1,0:T(8,128)}) fusion(bf16[256,16,128]{0,2,1:T(8,128)(2,1)} %bitcast.3, bf16[256,16,128]{2,1,0:T(8,128)(2,1)S(1)} %bitcast.155), kind=kOutput, calls=%fused_computation.12 | convolution fusion | flops 270528512 | bytes 6307840 | tf_op jit(solution)/shard_map/cqhd,ckhd->cqhk/dot_general | solution.py:47
  38.3 4.0 %bitcast_reduce_fusion.1 = (f32[256,16]{0,1:T(8,128)S(1)}, f32[16,256,256]{2,1,0:T(8,128)}) fusion(bf16[256,16,128]{0,2,1:T(8,128)(2,1)} %bitcast.6, bf16[256,16,128]{2,1,0:T(8,128)(2,1)S(1)} %bitcast.156), kind=kOutput, calls=%fused_computation.9 | convolution fusion | flops 270528512 | bytes 6307840 | tf_op jit(solution)/shard_map/cqhd,ckhd->cqhk/dot_general | solution.py:47
  42.3 4.0 %bitcast_reduce_fusion = (f32[256,16]{0,1:T(8,128)S(1)}, f32[16,256,256]{2,1,0:T(8,128)}) fusion(bf16[256,16,128]{0,2,1:T(8,128)(2,1)} %bitcast.9, bf16[256,16,128]{2,1,0:T(8,128)(2,1)S(1)} %bitcast.157), kind=kOutput, calls=%fused_computation.6 | convolution fusion | flops 270528512 | bytes 6307840 | tf_op jit(solution)/shard_map/cqhd,ckhd->cqhk/dot_general | solution.py:47
  46.3 12.8 %collective-permute-done.3 = bf16[1,256,2048]{2,1,0:T(8,128)(2,1)S(1)} collective-permute-done((bf16[1,256,2048]{2,1,0:T(8,128)(2,1)}, bf16[1,256,2048]{2,1,0:T(8,128)(2,1)S(1)}, u32[]{:S(2)}, u32[]{:S(2)}) %collective-permute-start.3) | collective-permute-done | bytes 1048608 | tf_op jit(solution)/shard_map/ppermute | solution.py:12
  60.7 3.6 %fusion.23 = f32[16,128,256]{2,1,0:T(8,128)S(1)} fusion(bf16[256,16,128]{0,2,1:T(8,128)(2,1)} %bitcast.161, f32[16,256,256]{2,1,0:T(8,128)} %get-tuple-element.30, f32[256,16]{0,1:T(8,128)S(1)} %maximum_maximum_fusion), kind=kOutput, calls=%fused_computation.41 | convolution fusion | flops 271581184 | bytes 7356416 | tf_op jit(solution)/shard_map/cqhk,ckhd->cqhd/dot_general | solution.py:64
  64.7 6.2 %fusion.6 = (f32[256,16]{0,1:T(8,128)S(1)}, f32[256,16]{0,1:T(8,128)S(1)}, f32[256,16]{0,1:T(8,128)S(1)}, f32[256,16]{0,1:T(8,128)S(1)}) fusion(f32[16,256,256]{2,1,0:T(8,128)} %get-tuple-element.30, f32[256,16]{0,1:T(8,128)S(1)} %maximum_maximum_fusion, f32[16,256,256]{2,1,0:T(8,128)S(1)} %copy-done, f32[16,256,256]{2,1,0:T(8,128)} %get-tuple-element.28, ...), kind=kLoop, calls=%fused_computation.19 | loop fusion | flops 12566528 | bytes 16859136 | tf_op jit(solution)/shard_map/reduce_sum | solution.py:63
  77.0 5.9 %bitcast_divide_fusion = f32[1,256,16,128]{1,3,2,0:T(8,128)} fusion(f32[16,256,128]{1,2,0:T(8,128)} %fusion.20, f32[16,128,256]{2,1,0:T(8,128)S(1)} %fusion.23, f32[16,256,128]{1,2,0:T(8,128)} %fusion.26, f32[256,16]{0,1:T(8,128)S(1)} %add_add_fusion, bf16[256,16,128]{0,2,1:T(8,128)(2,1)S(1)} %bitcast.164, f32[16,256,256]{2,1,0:T(8,128)} %get-tuple-element.26, ...), kind=kOutput, calls=%fused_computation.47 | convolution fusion | flops 273678336 | bytes 13664256 | tf_op jit(solution)/shard_map/cqhk,ckhd->cqhd/dot_general | solution.py:64
  86.6 21.5 %collective-permute-done.6 = bf16[2048,512]{1,0:T(8,128)(2,1)} collective-permute-done((bf16[2048,512]{1,0:T(8,128)(2,1)}, bf16[2048,512]{1,0:T(8,128)(2,1)}, u32[]{:S(2)}, u32[]{:S(2)}) %collective-permute-start.6) | collective-permute-done | bytes 2097184 | tf_op jit(solution)/shard_map/ppermute | solution.py:12
  108.0 4.1 %gather_fusion = bf16[640,2048]{1,0:T(8,128)(2,1)} fusion(bf16[256,2048]{1,0:T(8,128)(2,1)S(1)} %bitcast.153, s32[1024]{0:T(1024)S(1)} %pad_clamp_fusion.2), kind=kCustom, calls=%fused_computation | custom fusion | bytes 5245440 | tf_op jit(solution)/shard_map/gather | solution.py:95
  112.1 5.3 %reshape.341 = bf16[64,80,256]{2,1,0:T(8,128)(2,1)} reshape(bf16[640,2048]{1,0:T(8,128)(2,1)} %gather_fusion) | data formatting | bytes 5242880 | tf_op jit(solution)/shard_map/reshape | solution.py:96
  117.4 12.7 %all-to-all-start = ((bf16[64,80,256]{2,1,0:T(8,128)(2,1)}), bf16[64,80,256]{2,1,0:T(8,128)(2,1)S(1)}, u32[]{:S(2)}, u32[]{:S(2)}) async-start(bf16[64,80,256]{2,1,0:T(8,128)(2,1)} %reshape.341), calls=%async_computation | async-start | bytes 5242880 | tf_op jit(solution)/shard_map/all_to_all | solution.py:99
  131.6 44.3 %collective-permute-done.7 = bf16[256,2048]{1,0:T(8,128)(2,1)} collective-permute-done((bf16[256,2048]{1,0:T(8,128)(2,1)}, bf16[256,2048]{1,0:T(8,128)(2,1)}, u32[]{:S(2)}, u32[]{:S(2)}) %collective-permute-start.7) | collective-permute-done | bytes 1048608 | tf_op jit(solution)/shard_map/ppermute | solution.py:12
  175.9 15.7 %all-to-all-done = bf16[64,80,256]{2,1,0:T(8,128)(2,1)S(1)} async-done(((bf16[64,80,256]{2,1,0:T(8,128)(2,1)}), bf16[64,80,256]{2,1,0:T(8,128)(2,1)S(1)}, u32[]{:S(2)}, u32[]{:S(2)}) %all-to-all-start) | async-done | bytes 2621472 | tf_op jit(solution)/shard_map/all_to_all | solution.py:99
  191.5 3.1 %reshape.342 = bf16[640,2048]{1,0:T(8,128)(2,1)} reshape(bf16[64,80,256]{2,1,0:T(8,128)(2,1)S(1)} %all-to-all-done) | data formatting | bytes 5242880 | tf_op jit(solution)/shard_map/reshape | solution.py:100
  194.7 4.0 %fusion.82 = f32[640,512]{1,0:T(8,128)S(1)} fusion(bf16[640,2048]{1,0:T(8,128)(2,1)} %reshape.342, bf16[2048,512]{1,0:T(8,128)(2,1)} %collective-permute-done.6), kind=kOutput, calls=%fused_computation.124 | convolution fusion | flops 1342177280 | bytes 6029312 | tf_op jit(solution)/shard_map/dot_general | solution.py:103
  198.7 3.2 %fusion.81 = f32[640,512]{1,0:T(8,128)S(1)} fusion(bf16[640,2048]{1,0:T(8,128)(2,1)S(1)} %copy-done.6, bf16[2048,512]{1,0:T(8,128)(2,1)} %bitcast.52), kind=kOutput, calls=%fused_computation.123 | convolution fusion | flops 1342177280 | bytes 6029312 | tf_op jit(solution)/shard_map/dot_general | solution.py:103
  202.9 3.1 %fusion.83 = f32[640,512]{1,0:T(8,128)S(1)} fusion(bf16[640,2048]{1,0:T(8,128)(2,1)S(1)} %copy-done.6, bf16[2048,512]{1,0:T(8,128)(2,1)} %collective-permute-done.8), kind=kOutput, calls=%fused_computation.125 | convolution fusion | flops 1342177280 | bytes 6029312 | tf_op jit(solution)/shard_map/dot_general | solution.py:103
  210.2 3.1 %fusion.84 = f32[640,512]{1,0:T(8,128)S(1)} fusion(bf16[640,2048]{1,0:T(8,128)(2,1)S(1)} %copy-done.6, bf16[2048,512]{1,0:T(8,128)(2,1)} %collective-permute-done.10), kind=kOutput, calls=%fused_computation.126 | convolution fusion | flops 1342177280 | bytes 6029312 | tf_op jit(solution)/shard_map/dot_general | solution.py:103
  216.0 3.2 %reshape.343 = bf16[64,80,256]{2,1,0:T(8,128)(2,1)} reshape(bf16[640,2048]{1,0:T(8,128)(2,1)S(1)} %add_convert_fusion) | data formatting | bytes 5242880 | tf_op jit(solution)/shard_map/reshape | solution.py:110
  219.2 6.5 %all-to-all-start.1 = ((bf16[64,80,256]{2,1,0:T(8,128)(2,1)}), bf16[64,80,256]{2,1,0:T(8,128)(2,1)}, u32[]{:S(2)}, u32[]{:S(2)}) async-start(bf16[64,80,256]{2,1,0:T(8,128)(2,1)} %reshape.343), calls=%async_computation.1 | async-start | bytes 5242880 | tf_op jit(solution)/shard_map/all_to_all | solution.py:111
  226.1 60.8 %all-to-all-done.1 = bf16[64,80,256]{2,1,0:T(8,128)(2,1)} async-done(((bf16[64,80,256]{2,1,0:T(8,128)(2,1)}), bf16[64,80,256]{2,1,0:T(8,128)(2,1)}, u32[]{:S(2)}, u32[]{:S(2)}) %all-to-all-start.1) | async-done | bytes 2621472 | tf_op jit(solution)/shard_map/all_to_all | solution.py:111
  286.9 3.9 %reshape.344 = bf16[640,2048]{1,0:T(8,128)(2,1)S(1)} reshape(bf16[64,80,256]{2,1,0:T(8,128)(2,1)} %all-to-all-done.1) | data formatting | bytes 5242880 | tf_op jit(solution)/shard_map/reshape | solution.py:112
  295.6 3.4 %fusion.15 = bf16[1,256,2048]{2,1,0:T(8,128)(2,1)} fusion(bf16[1,256,2048]{2,1,0:T(8,128)(2,1)} %copy-done.2, bf16[256,2048]{1,0:T(8,128)(2,1)} %gather_fusion.2, bf16[256,2048]{1,0:T(8,128)(2,1)} %gather_fusion.1, f32[256]{0:T(256)S(1)} %bitcast.169, f32[256]{0:T(256)S(1)} %bitcast.168), kind=kLoop, calls=%fused_computation.35 | loop fusion | flops 4194304 | bytes 4196352 | tf_op jit(solution)/shard_map/convert_element_type | solution.py:119
  (93 shorter events, 47.8 us)
Async XLA Ops:
  2.3 26.7 %collective-permute-start = (bf16[1,256,2048]{1,2,0:T(8,128)(2,1)}, bf16[1,256,2048]{1,2,0:T(8,128)(2,1)}, u32[]{:S(2)}, u32[]{:S(2)}) collective-permute-start(bf16[1,256,2048]{1,2,0:T(8,128)(2,1)} %copy.49), channel_id=1, source_target_pairs={{0,128},{64,192},{128,0},{192,64},{1,129},{65,193},{129,1},{193,65... | collective-permute-start | bytes 3145736 | tf_op jit(solution)/shard_map/ppermute | solution.py:12
  4.5 33.8 %collective-permute-start.1 = (bf16[1,256,2048]{1,2,0:T(8,128)(2,1)}, bf16[1,256,2048]{1,2,0:T(8,128)(2,1)}, u32[]{:S(2)}, u32[]{:S(2)}) collective-permute-start(bf16[1,256,2048]{1,2,0:T(8,128)(2,1)} %copy.49), channel_id=1, source_target_pairs={{0,64},{64,0},{128,192},{192,128},{1,65},{65,1},{129,193},{193,129... | collective-permute-start | bytes 3145736 | tf_op jit(solution)/shard_map/ppermute | solution.py:17
  4.5 27.5 %collective-permute-start.4 = (bf16[1,256,2048]{2,1,0:T(8,128)(2,1)}, bf16[1,256,2048]{2,1,0:T(8,128)(2,1)}, u32[]{:S(2)}, u32[]{:S(2)}) collective-permute-start(bf16[1,256,2048]{2,1,0:T(8,128)(2,1)} %param.11), channel_id=1, source_target_pairs={{0,64},{64,0},{128,192},{192,128},{1,65},{65,1},{129,193},{193,129... | collective-permute-start | bytes 3145736 | tf_op jit(solution)/shard_map/ppermute | solution.py:17
  5.8 4.9 %copy-start.4 = (bf16[1,256,2048]{2,1,0:T(8,128)(2,1)S(1)}, bf16[1,256,2048]{2,1,0:T(8,128)(2,1)}, u32[]{:S(2)}) copy-start(bf16[1,256,2048]{2,1,0:T(8,128)(2,1)} %param.10) | copy-start | bytes 3145732
  9.1 2.8 copy-start.7
  11.9 17.1 %copy-start.5 = (bf16[32,8,16,128]{3,2,1,0:T(8,128)(2,1)S(1)}, bf16[32,8,16,128]{3,2,1,0:T(8,128)(2,1)}, u32[]{:S(2)}) copy-start(bf16[32,8,16,128]{3,2,1,0:T(8,128)(2,1)} %copy.79) | copy-start | bytes 3145732
  29.0 13.3 %collective-permute-start.2 = (bf16[1,256,2048]{1,2,0:T(8,128)(2,1)}, bf16[1,256,2048]{1,2,0:T(8,128)(2,1)}, u32[]{:S(2)}, u32[]{:S(2)}) collective-permute-start(bf16[1,256,2048]{1,2,0:T(8,128)(2,1)} %collective-permute-done), channel_id=1, source_target_pairs={{0,64},{64,0},{128,192},{192,128},{1,65},{65,1},{129,193},{193,129... | collective-permute-start | bytes 3145736 | tf_op jit(solution)/shard_map/ppermute | solution.py:17
  31.7 27.3 %collective-permute-start.3 = (bf16[1,256,2048]{2,1,0:T(8,128)(2,1)}, bf16[1,256,2048]{2,1,0:T(8,128)(2,1)S(1)}, u32[]{:S(2)}, u32[]{:S(2)}) collective-permute-start(bf16[1,256,2048]{2,1,0:T(8,128)(2,1)} %param.11), channel_id=1, source_target_pairs={{0,128},{64,192},{128,0},{192,64},{1,129},{65,193},{129,1},{193,65... | collective-permute-start | bytes 3145736 | tf_op jit(solution)/shard_map/ppermute | solution.py:12
  59.0 49.0 %collective-permute-start.6 = (bf16[2048,512]{1,0:T(8,128)(2,1)}, bf16[2048,512]{1,0:T(8,128)(2,1)}, u32[]{:S(2)}, u32[]{:S(2)}) collective-permute-start(bf16[2048,512]{1,0:T(8,128)(2,1)} %bitcast.52), channel_id=1, source_target_pairs={{0,128},{64,192},{128,0},{192,64},{1,129},{65,193},{129,1},{193,65... | collective-permute-start | bytes 6291464 | tf_op jit(solution)/shard_map/ppermute | solution.py:12
  60.7 3.6 %copy-start.10 = (bf16[1,256,2048]{2,1,0:T(8,128)(2,1)S(1)}, bf16[1,256,2048]{2,1,0:T(8,128)(2,1)}, u32[]{:S(2)}) copy-start(bf16[1,256,2048]{2,1,0:T(8,128)(2,1)} %copy-done.9) | copy-start | bytes 3145732
  60.7 4.1 %copy-start = (f32[16,256,256]{2,1,0:T(8,128)S(1)}, f32[16,256,256]{2,1,0:T(8,128)}, u32[]{:S(2)}) copy-start(f32[16,256,256]{2,1,0:T(8,128)} %get-tuple-element.32) | copy-start | bytes 12582916
  64.2 11.3 %collective-permute-start.5 = (bf16[1,256,2048]{2,1,0:T(8,128)(2,1)S(1)}, bf16[1,256,2048]{2,1,0:T(8,128)(2,1)}, u32[]{:S(2)}, u32[]{:S(2)}) collective-permute-start(bf16[1,256,2048]{2,1,0:T(8,128)(2,1)S(1)} %copy-done.10), channel_id=1, source_target_pairs={{0,64},{64,0},{128,192},{192,128},{1,65},{65,1},{129,193},{193,129... | collective-permute-start | bytes 3145736 | tf_op jit(solution)/shard_map/ppermute | solution.py:17
  64.7 6.2 %copy-start.1 = (f32[16,256,256]{2,1,0:T(8,128)S(1)}, f32[16,256,256]{2,1,0:T(8,128)}, u32[]{:S(2)}) copy-start(f32[16,256,256]{2,1,0:T(8,128)} %get-tuple-element.28) | copy-start | bytes 12582916
  64.7 6.3 %copy-start.3 = (bf16[1,256,2048]{1,2,0:T(8,128)(2,1)S(1)}, bf16[1,256,2048]{1,2,0:T(8,128)(2,1)}, u32[]{:S(2)}) copy-start(bf16[1,256,2048]{1,2,0:T(8,128)(2,1)} %copy.61) | copy-start | bytes 3145732
  117.4 74.1 %all-to-all-start = ((bf16[64,80,256]{2,1,0:T(8,128)(2,1)}), bf16[64,80,256]{2,1,0:T(8,128)(2,1)S(1)}, u32[]{:S(2)}, u32[]{:S(2)}) async-start(bf16[64,80,256]{2,1,0:T(8,128)(2,1)} %reshape.341), calls=%async_computation | async-start | bytes 5242880 | tf_op jit(solution)/shard_map/all_to_all | solution.py:99
  130.1 45.7 %collective-permute-start.7 = (bf16[256,2048]{1,0:T(8,128)(2,1)}, bf16[256,2048]{1,0:T(8,128)(2,1)}, u32[]{:S(2)}, u32[]{:S(2)}) collective-permute-start(bf16[256,2048]{1,0:T(8,128)(2,1)} %bitcast.172), channel_id=1, source_target_pairs={{0,128},{64,192},{128,0},{192,64},{1,129},{65,193},{129,1},{193,65... | collective-permute-start | bytes 3145736 | tf_op jit(solution)/shard_map/ppermute | solution.py:12
  131.0 71.8 %collective-permute-start.8 = (bf16[2048,512]{1,0:T(8,128)(2,1)}, bf16[2048,512]{1,0:T(8,128)(2,1)}, u32[]{:S(2)}, u32[]{:S(2)}) collective-permute-start(bf16[2048,512]{1,0:T(8,128)(2,1)} %bitcast.52), channel_id=1, source_target_pairs={{0,64},{64,0},{128,192},{192,128},{1,65},{65,1},{129,193},{193,129... | collective-permute-start | bytes 6291464 | tf_op jit(solution)/shard_map/ppermute | solution.py:17
  131.0 77.0 %collective-permute-start.9 = (bf16[256,2048]{1,0:T(8,128)(2,1)}, bf16[256,2048]{1,0:T(8,128)(2,1)}, u32[]{:S(2)}, u32[]{:S(2)}) collective-permute-start(bf16[256,2048]{1,0:T(8,128)(2,1)} %bitcast.173), channel_id=1, source_target_pairs={{0,64},{64,0},{128,192},{192,128},{1,65},{65,1},{129,193},{193,129... | collective-permute-start | bytes 3145736 | tf_op jit(solution)/shard_map/ppermute | solution.py:17
  131.5 78.7 %collective-permute-start.10 = (bf16[2048,512]{1,0:T(8,128)(2,1)}, bf16[2048,512]{1,0:T(8,128)(2,1)}, u32[]{:S(2)}, u32[]{:S(2)}) collective-permute-start(bf16[2048,512]{1,0:T(8,128)(2,1)} %collective-permute-done.6), channel_id=1, source_target_pairs={{0,64},{64,0},{128,192},{192,128},{1,65},{65,1},{129,193},{193,129... | collective-permute-start | bytes 6291464 | tf_op jit(solution)/shard_map/ppermute | solution.py:17
  175.9 37.4 %collective-permute-start.11 = (bf16[256,2048]{1,0:T(8,128)(2,1)}, bf16[256,2048]{1,0:T(8,128)(2,1)}, u32[]{:S(2)}, u32[]{:S(2)}) collective-permute-start(bf16[256,2048]{1,0:T(8,128)(2,1)} %collective-permute-done.7), channel_id=1, source_target_pairs={{0,64},{64,0},{128,192},{192,128},{1,65},{65,1},{129,193},{193,129... | collective-permute-start | bytes 3145736 | tf_op jit(solution)/shard_map/ppermute | solution.py:17
  194.7 4.0 %copy-start.6 = (bf16[640,2048]{1,0:T(8,128)(2,1)S(1)}, bf16[640,2048]{1,0:T(8,128)(2,1)}, u32[]{:S(2)}) copy-start(bf16[640,2048]{1,0:T(8,128)(2,1)} %reshape.342) | copy-start | bytes 7864324
  198.7 3.2 %copy-start.13 = (bf16[1,256,2048]{2,1,0:T(8,128)(2,1)S(1)}, bf16[1,256,2048]{2,1,0:T(8,128)(2,1)}, u32[]{:S(2)}) copy-start(bf16[1,256,2048]{2,1,0:T(8,128)(2,1)} %param.17) | copy-start | bytes 3145732
  219.2 6.9 %copy-start.12 = (f32[1,256,2]{1,2,0:T(2,128)S(1)}, f32[1,256,2]{1,2,0:T(2,128)}, u32[]{:S(2)}) copy-start(f32[1,256,2]{1,2,0:T(2,128)} %param.15) | copy-start | bytes 6148
  219.2 67.8 %all-to-all-start.1 = ((bf16[64,80,256]{2,1,0:T(8,128)(2,1)}), bf16[64,80,256]{2,1,0:T(8,128)(2,1)}, u32[]{:S(2)}, u32[]{:S(2)}) async-start(bf16[64,80,256]{2,1,0:T(8,128)(2,1)} %reshape.343), calls=%async_computation.1 | async-start | bytes 5242880 | tf_op jit(solution)/shard_map/all_to_all | solution.py:111
  (4 other events, 6.0 us)
where the time goes:
time: 300 us; the launch traced here: 299 us
  waiting for transfers between devices  167 us (56%)
  matrix products  49.8 us (17%)
  local copies, waits for them, and re-layouts  45.1 us (15%)
  starting transfers between devices  24.2 us (8%)
  other arithmetic  12 us (4%)
    ppermute x4, waiting for transfers between devices, far_block(): return lax.ppermute(block, 'ctx', perm=[(c, c ^ 2) for c in range(4)])  91 us
    all_to_all x1, waiting for transfers between devices, shards(): lax.all_to_all(summed, 'exp', split_axis=0, concat_axis=0, tiled=True)  60.8 us
    all_to_all x1, waiting for transfers between devices, shards(): lax.all_to_all(send_buffer, 'exp', split_axis=0, concat_axis=0, tiled=True)  15.7 us
    dot_general x4, matrix products, shards(): jnp.einsum('cqhd,ckhd->cqhk', query_heads, block.reshape(clip_count, -1,...  14.7 us
    dot_general x4, matrix products, shards(): jnp.einsum('cqhk,ckhd->cqhd', expo.astype(jnp.bfloat16), block.reshape(cl...  13.9 us
    dot_general x4, matrix products, shards(): jnp.dot(flattened, gate_up_block, preferred_element_type=jnp.float32)  13.4 us
    all_to_all x1, starting transfers between devices, shards(): lax.all_to_all(send_buffer, 'exp', split_axis=0, concat_axis=0, tiled=True)  12.7 us
    unnamed x33, local copies, waits for them, and re-layouts  8.98 us
  transfers between devices with their start and end apart: 14, of which 6 were waited for; matrix products, arithmetic and copies ran while one was open for 25% of the time, Pallas kernels for 0%

commit v1 on v0

--- a/solution.py
+++ b/solution.py
@@ -39,8 +39,8 @@
     down_local = down_weight[0]
     key_far = far_block(key_rows)
     value_far = far_block(value_rows, key_far)
-    gate_up_far = far_block(gate_up_local, value_far)
-    down_far = far_block(down_local, gate_up_far)
+    down_far = far_block(down_local, value_far)
+    gate_up_far = far_block(gate_up_local, down_far)
     key_blocks = near_blocks(key_rows, key_far)
     value_blocks = near_blocks(value_rows, value_far)
     block_scores = [
@@ -91,7 +91,7 @@
         .at[destination]
         .set(jnp.arange(token_count * top_count, dtype=jnp.int32) // top_count)
     )
-    normed, gate_up_far = lax.optimization_barrier((normed, gate_up_far))
+    normed, down_far = lax.optimization_barrier((normed, down_far))
     send_buffer = normed.reshape(token_count, feature_count)[slot_token]
     send_buffer = send_buffer.reshape(expert_count, capacity * 8, feature_count // 8)
     gate_up_blocks = near_blocks(gate_up_local, gate_up_far)

time: 300 us -> 304 us (1.013)
  starting transfers between devices: 24.2 us -> 30.8 us
  waiting for transfers between devices: 167 us -> 162 us
    all_to_all x1, waiting for transfers between devices: 15.7 us -> 0.01 us  [shards(): lax.all_to_all(send_buffer, 'exp', split_axis=0, concat_axis=0, tiled=True)]
    ppermute x4, waiting for transfers between devices: 91 us -> 98.7 us  [far_block(): return lax.ppermute(block, 'ctx', perm=[(c, c ^ 2) for c in range(4)])]
    all_to_all x1, starting transfers between devices: 6.52 us -> 11.3 us  [shards(): lax.all_to_all(summed, 'exp', split_axis=0, concat_axis=0, tiled=True)]
    unnamed x33 -> x27, local copies, waits for them, and re-layouts: 8.98 us -> 10.2 us
  transfers between devices with their start and end apart: 14 -> 14, of which waited for: 6 -> 4; matrix products, arithmetic and copies ran while one was open for 25% -> 26% of each run, Pallas kernels for 0% -> 0%
where the time goes in v1:
time: 304 us; the launch traced here: 303 us
  waiting for transfers between devices  162 us (53%)
  matrix products  52.3 us (17%)
  local copies, waits for them, and re-layouts  46.3 us (15%)
  starting transfers between devices  30.8 us (10%)
  other arithmetic  12 us (4%)
    ppermute x4, waiting for transfers between devices, far_block(): return lax.ppermute(block, 'ctx', perm=[(c, c ^ 2) for c in range(4)])  98.7 us
    all_to_all x1, waiting for transfers between devices, shards(): lax.all_to_all(summed, 'exp', split_axis=0, concat_axis=0, tiled=True)  62.8 us
    dot_general x4, matrix products, shards(): jnp.einsum('cqhd,ckhd->cqhk', query_heads, block.reshape(clip_count, -1,...  16 us
    dot_general x4, matrix products, shards(): jnp.einsum('cqhk,ckhd->cqhd', expo.astype(jnp.bfloat16), block.reshape(cl...  13.9 us
    all_to_all x1, starting transfers between devices, shards(): lax.all_to_all(send_buffer, 'exp', split_axis=0, concat_axis=0, tiled=True)  13.9 us
    dot_general x4, matrix products, shards(): jnp.dot(flattened, gate_up_block, preferred_element_type=jnp.float32)  13.3 us
    all_to_all x1, starting transfers between devices, shards(): lax.all_to_all(summed, 'exp', split_axis=0, concat_axis=0, tiled=True)  11.3 us
    unnamed x27, local copies, waits for them, and re-layouts  10.2 us
  transfers between devices with their start and end apart: 14, of which 4 were waited for; matrix products, arithmetic and copies ran while one was open for 26% of the time, Pallas kernels for 0%

profile of v1, /device:TPU:4, one launch (start us, length us, event | category | flops | bytes accessed | tf_op | source)
XLA Modules:
  0.0 303.3 jit_solution(9459766179526467680)
XLA Ops:
  13.7 15.4 %collective-permute-done = bf16[1,256,2048]{1,2,0:T(8,128)(2,1)} collective-permute-done((bf16[1,256,2048]{1,2,0:T(8,128)(2,1)}, bf16[1,256,2048]{1,2,0:T(8,128)(2,1)}, u32[]{:S(2)}, u32[]{:S(2)}) %collective-permute-start) | collective-permute-done | bytes 1048608 | tf_op jit(solution)/shard_map/ppermute | solution.py:12
  29.1 4.0 %bitcast_reduce_fusion.3 = (f32[256,16]{0,1:T(8,128)S(1)}, f32[16,256,256]{2,1,0:T(8,128)}) fusion(bf16[256,16,128]{2,1,0:T(8,128)(2,1)S(1)} %bitcast.154, bf16[256,16,128]{2,1,0:T(8,128)(2,1)} %bitcast.163), kind=kOutput, calls=%fused_computation.15 | convolution fusion | flops 270528512 | bytes 6307840 | tf_op jit(solution)/shard_map/cqhd,ckhd->cqhk/dot_general | solution.py:47
  35.7 4.0 %bitcast_reduce_fusion.2 = (f32[256,16]{0,1:T(8,128)S(1)}, f32[16,256,256]{2,1,0:T(8,128)}) fusion(bf16[256,16,128]{0,2,1:T(8,128)(2,1)} %bitcast.3, bf16[256,16,128]{2,1,0:T(8,128)(2,1)S(1)} %bitcast.155), kind=kOutput, calls=%fused_computation.12 | convolution fusion | flops 270528512 | bytes 6307840 | tf_op jit(solution)/shard_map/cqhd,ckhd->cqhk/dot_general | solution.py:47
  39.7 4.0 %bitcast_reduce_fusion.1 = (f32[256,16]{0,1:T(8,128)S(1)}, f32[16,256,256]{2,1,0:T(8,128)}) fusion(bf16[256,16,128]{0,2,1:T(8,128)(2,1)} %bitcast.6, bf16[256,16,128]{2,1,0:T(8,128)(2,1)S(1)} %bitcast.156), kind=kOutput, calls=%fused_computation.9 | convolution fusion | flops 270528512 | bytes 6307840 | tf_op jit(solution)/shard_map/cqhd,ckhd->cqhk/dot_general | solution.py:47
  43.7 4.0 %bitcast_reduce_fusion = (f32[256,16]{0,1:T(8,128)S(1)}, f32[16,256,256]{2,1,0:T(8,128)}) fusion(bf16[256,16,128]{0,2,1:T(8,128)(2,1)} %bitcast.9, bf16[256,16,128]{2,1,0:T(8,128)(2,1)S(1)} %bitcast.157), kind=kOutput, calls=%fused_computation.6 | convolution fusion | flops 270528512 | bytes 6307840 | tf_op jit(solution)/shard_map/cqhd,ckhd->cqhk/dot_general | solution.py:47
  47.7 12.7 %collective-permute-done.3 = bf16[1,256,2048]{2,1,0:T(8,128)(2,1)} collective-permute-done((bf16[1,256,2048]{2,1,0:T(8,128)(2,1)S(1)}, bf16[1,256,2048]{2,1,0:T(8,128)(2,1)}, u32[]{:S(2)}, u32[]{:S(2)}) %collective-permute-start.3) | collective-permute-done | bytes 1048608 | tf_op jit(solution)/shard_map/ppermute | solution.py:12
  62.9 3.6 %fusion.23 = f32[16,128,256]{2,1,0:T(8,128)S(1)} fusion(bf16[256,16,128]{0,2,1:T(8,128)(2,1)} %bitcast.161, f32[16,256,256]{2,1,0:T(8,128)} %get-tuple-element.30, f32[256,16]{0,1:T(8,128)S(1)} %maximum_maximum_fusion), kind=kOutput, calls=%fused_computation.41 | convolution fusion | flops 271581184 | bytes 7356416 | tf_op jit(solution)/shard_map/cqhk,ckhd->cqhd/dot_general | solution.py:64
  66.8 6.2 %fusion.6 = (f32[256,16]{0,1:T(8,128)S(1)}, f32[256,16]{0,1:T(8,128)S(1)}, f32[256,16]{0,1:T(8,128)S(1)}, f32[256,16]{0,1:T(8,128)S(1)}) fusion(f32[16,256,256]{2,1,0:T(8,128)} %get-tuple-element.30, f32[256,16]{0,1:T(8,128)S(1)} %maximum_maximum_fusion, f32[16,256,256]{2,1,0:T(8,128)S(1)} %copy-done, f32[16,256,256]{2,1,0:T(8,128)} %get-tuple-element.28, ...), kind=kLoop, calls=%fused_computation.19 | loop fusion | flops 12566528 | bytes 16859136 | tf_op jit(solution)/shard_map/reduce_sum | solution.py:63
  79.1 5.9 %bitcast_divide_fusion = f32[1,256,16,128]{1,3,2,0:T(8,128)} fusion(f32[16,256,128]{1,2,0:T(8,128)} %fusion.20, f32[16,128,256]{2,1,0:T(8,128)S(1)} %fusion.23, f32[16,256,128]{1,2,0:T(8,128)} %fusion.26, f32[256,16]{0,1:T(8,128)S(1)} %add_add_fusion, bf16[256,16,128]{0,2,1:T(8,128)(2,1)S(1)} %bitcast.164, f32[16,256,256]{2,1,0:T(8,128)} %get-tuple-element.26, ...), kind=kOutput, calls=%fused_computation.47 | convolution fusion | flops 273678336 | bytes 13664256 | tf_op jit(solution)/shard_map/cqhk,ckhd->cqhd/dot_general | solution.py:64
  88.6 4.1 %gather_fusion = bf16[640,2048]{1,0:T(8,128)(2,1)} fusion(bf16[256,2048]{1,0:T(8,128)(2,1)S(1)} %bitcast.153, s32[1024]{0:T(1024)S(1)} %pad_clamp_fusion.2), kind=kCustom, calls=%fused_computation | custom fusion | bytes 5245440 | tf_op jit(solution)/shard_map/gather | solution.py:95
  92.7 5.3 %reshape.341 = bf16[64,80,256]{2,1,0:T(8,128)(2,1)} reshape(bf16[640,2048]{1,0:T(8,128)(2,1)} %gather_fusion) | data formatting | bytes 5242880 | tf_op jit(solution)/shard_map/reshape | solution.py:96
  98.0 13.9 %all-to-all-start = ((bf16[64,80,256]{2,1,0:T(8,128)(2,1)}), bf16[64,80,256]{2,1,0:T(8,128)(2,1)S(1)}, u32[]{:S(2)}, u32[]{:S(2)}) async-start(bf16[64,80,256]{2,1,0:T(8,128)(2,1)} %reshape.341), calls=%async_computation | async-start | bytes 5242880 | tf_op jit(solution)/shard_map/all_to_all | solution.py:99
  111.9 3.4 %copy.81 = bf16[256,8,2,256]{3,1,2,0:T(8,128)(2,1)} copy(bf16[256,8,2,256]{3,2,1,0:T(2,128)(2,1)} %bitcast.165) | data formatting | bytes 4194304
  117.3 70.6 %collective-permute-done.7 = bf16[2048,512]{1,0:T(8,128)(2,1)} collective-permute-done((bf16[2048,512]{1,0:T(8,128)(2,1)}, bf16[2048,512]{1,0:T(8,128)(2,1)}, u32[]{:S(2)}, u32[]{:S(2)}) %collective-permute-start.7) | collective-permute-done | bytes 2097184 | tf_op jit(solution)/shard_map/ppermute | solution.py:12
  187.9 3.1 %reshape.342 = bf16[640,2048]{1,0:T(8,128)(2,1)} reshape(bf16[64,80,256]{2,1,0:T(8,128)(2,1)S(1)} %all-to-all-done) | data formatting | bytes 5242880 | tf_op jit(solution)/shard_map/reshape | solution.py:100
  191.1 4.0 %fusion.81 = f32[640,512]{1,0:T(8,128)S(1)} fusion(bf16[640,2048]{1,0:T(8,128)(2,1)} %reshape.342, bf16[2048,512]{1,0:T(8,128)(2,1)} %bitcast.52), kind=kOutput, calls=%fused_computation.123 | convolution fusion | flops 1342177280 | bytes 6029312 | tf_op jit(solution)/shard_map/dot_general | solution.py:103
  195.1 3.1 %fusion.82 = f32[640,512]{1,0:T(8,128)S(1)} fusion(bf16[640,2048]{1,0:T(8,128)(2,1)S(1)} %copy-done.5, bf16[2048,512]{1,0:T(8,128)(2,1)} %collective-permute-done.7), kind=kOutput, calls=%fused_computation.124 | convolution fusion | flops 1342177280 | bytes 6029312 | tf_op jit(solution)/shard_map/dot_general | solution.py:103
  200.4 3.1 %fusion.83 = f32[640,512]{1,0:T(8,128)S(1)} fusion(bf16[640,2048]{1,0:T(8,128)(2,1)S(1)} %copy-done.5, bf16[2048,512]{1,0:T(8,128)(2,1)} %collective-permute-done.8), kind=kOutput, calls=%fused_computation.125 | convolution fusion | flops 1342177280 | bytes 6029312 | tf_op jit(solution)/shard_map/dot_general | solution.py:103
  207.7 3.1 %fusion.84 = f32[640,512]{1,0:T(8,128)S(1)} fusion(bf16[640,2048]{1,0:T(8,128)(2,1)S(1)} %copy-done.5, bf16[2048,512]{1,0:T(8,128)(2,1)} %collective-permute-done.10), kind=kOutput, calls=%fused_computation.126 | convolution fusion | flops 1342177280 | bytes 6029312 | tf_op jit(solution)/shard_map/dot_general | solution.py:103
  213.5 3.2 %reshape.343 = bf16[64,80,256]{2,1,0:T(8,128)(2,1)} reshape(bf16[640,2048]{1,0:T(8,128)(2,1)S(1)} %add_convert_fusion) | data formatting | bytes 5242880 | tf_op jit(solution)/shard_map/reshape | solution.py:110
  216.7 11.3 %all-to-all-start.1 = ((bf16[64,80,256]{2,1,0:T(8,128)(2,1)}), bf16[64,80,256]{2,1,0:T(8,128)(2,1)}, u32[]{:S(2)}, u32[]{:S(2)}) async-start(bf16[64,80,256]{2,1,0:T(8,128)(2,1)} %reshape.343), calls=%async_computation.1 | async-start | bytes 5242880 | tf_op jit(solution)/shard_map/all_to_all | solution.py:111
  228.4 62.8 %all-to-all-done.1 = bf16[64,80,256]{2,1,0:T(8,128)(2,1)} async-done(((bf16[64,80,256]{2,1,0:T(8,128)(2,1)}), bf16[64,80,256]{2,1,0:T(8,128)(2,1)}, u32[]{:S(2)}, u32[]{:S(2)}) %all-to-all-start.1) | async-done | bytes 2621472 | tf_op jit(solution)/shard_map/all_to_all | solution.py:111
  291.3 3.9 %reshape.344 = bf16[640,2048]{1,0:T(8,128)(2,1)S(1)} reshape(bf16[64,80,256]{2,1,0:T(8,128)(2,1)} %all-to-all-done.1) | data formatting | bytes 5242880 | tf_op jit(solution)/shard_map/reshape | solution.py:112
  299.9 3.4 %fusion.15 = bf16[1,256,2048]{2,1,0:T(8,128)(2,1)} fusion(bf16[1,256,2048]{2,1,0:T(8,128)(2,1)} %copy-done.2, bf16[256,2048]{1,0:T(8,128)(2,1)} %gather_fusion.2, bf16[256,2048]{1,0:T(8,128)(2,1)} %gather_fusion.1, f32[256]{0:T(256)S(1)} %bitcast.169, f32[256]{0:T(256)S(1)} %bitcast.168), kind=kLoop, calls=%fused_computation.35 | loop fusion | flops 4194304 | bytes 4196352 | tf_op jit(solution)/shard_map/convert_element_type | solution.py:119
  (87 shorter events, 44.8 us)
Async XLA Ops:
  0.0 7.5 %copy-start.7 = (bf16[1,256,2048]{2,1,0:T(8,128)(2,1)S(1)}, bf16[1,256,2048]{2,1,0:T(8,128)(2,1)}, u32[]{:S(2)}) copy-start(bf16[1,256,2048]{2,1,0:T(8,128)(2,1)} %param.11) | copy-start | bytes 3145732
  2.4 26.7 %collective-permute-start = (bf16[1,256,2048]{1,2,0:T(8,128)(2,1)}, bf16[1,256,2048]{1,2,0:T(8,128)(2,1)}, u32[]{:S(2)}, u32[]{:S(2)}) collective-permute-start(bf16[1,256,2048]{1,2,0:T(8,128)(2,1)} %copy.49), channel_id=1, source_target_pairs={{0,128},{64,192},{128,0},{192,64},{1,129},{65,193},{129,1},{193,65... | collective-permute-start | bytes 3145736 | tf_op jit(solution)/shard_map/ppermute | solution.py:12
  4.6 35.1 %collective-permute-start.1 = (bf16[1,256,2048]{1,2,0:T(8,128)(2,1)}, bf16[1,256,2048]{1,2,0:T(8,128)(2,1)}, u32[]{:S(2)}, u32[]{:S(2)}) collective-permute-start(bf16[1,256,2048]{1,2,0:T(8,128)(2,1)} %copy.49), channel_id=1, source_target_pairs={{0,64},{64,0},{128,192},{192,128},{1,65},{65,1},{129,193},{193,129... | collective-permute-start | bytes 3145736 | tf_op jit(solution)/shard_map/ppermute | solution.py:17
  4.6 28.8 %collective-permute-start.4 = (bf16[1,256,2048]{2,1,0:T(8,128)(2,1)}, bf16[1,256,2048]{2,1,0:T(8,128)(2,1)}, u32[]{:S(2)}, u32[]{:S(2)}) collective-permute-start(bf16[1,256,2048]{2,1,0:T(8,128)(2,1)} %param.11), channel_id=1, source_target_pairs={{0,64},{64,0},{128,192},{192,128},{1,65},{65,1},{129,193},{193,129... | collective-permute-start | bytes 3145736 | tf_op jit(solution)/shard_map/ppermute | solution.py:17
  5.9 3.8 %copy-start.4 = (bf16[1,256,2048]{2,1,0:T(8,128)(2,1)S(1)}, bf16[1,256,2048]{2,1,0:T(8,128)(2,1)}, u32[]{:S(2)}) copy-start(bf16[1,256,2048]{2,1,0:T(8,128)(2,1)} %param.10) | copy-start | bytes 3145732
  29.1 14.6 %collective-permute-start.2 = (bf16[1,256,2048]{1,2,0:T(8,128)(2,1)}, bf16[1,256,2048]{1,2,0:T(8,128)(2,1)}, u32[]{:S(2)}, u32[]{:S(2)}) collective-permute-start(bf16[1,256,2048]{1,2,0:T(8,128)(2,1)} %collective-permute-done), channel_id=1, source_target_pairs={{0,64},{64,0},{128,192},{192,128},{1,65},{65,1},{129,193},{193,129... | collective-permute-start | bytes 3145736 | tf_op jit(solution)/shard_map/ppermute | solution.py:17
  29.1 4.1 %copy-start.8 = (bf16[1,256,2048]{2,1,0:T(8,128)(2,1)S(1)}, bf16[1,256,2048]{2,1,0:T(8,128)(2,1)}, u32[]{:S(2)}) copy-start(bf16[1,256,2048]{2,1,0:T(8,128)(2,1)} %param.11) | copy-start | bytes 3145732
  33.1 27.2 %collective-permute-start.3 = (bf16[1,256,2048]{2,1,0:T(8,128)(2,1)S(1)}, bf16[1,256,2048]{2,1,0:T(8,128)(2,1)}, u32[]{:S(2)}, u32[]{:S(2)}) collective-permute-start(bf16[1,256,2048]{2,1,0:T(8,128)(2,1)S(1)} %copy-done.8), channel_id=1, source_target_pairs={{0,128},{64,192},{128,0},{192,64},{1,129},{65,193},{129,1},{193,65... | collective-permute-start | bytes 3145736 | tf_op jit(solution)/shard_map/ppermute | solution.py:12
  60.3 28.3 %collective-permute-start.6 = (bf16[256,2048]{1,0:T(8,128)(2,1)}, bf16[256,2048]{1,0:T(8,128)(2,1)}, u32[]{:S(2)}, u32[]{:S(2)}) collective-permute-start(bf16[256,2048]{1,0:T(8,128)(2,1)} %bitcast.30), channel_id=1, source_target_pairs={{0,128},{64,192},{128,0},{192,64},{1,129},{65,193},{129,1},{193,65... | collective-permute-start | bytes 3145736 | tf_op jit(solution)/shard_map/ppermute | solution.py:12
  62.9 3.8 %copy-start = (f32[16,256,256]{2,1,0:T(8,128)S(1)}, f32[16,256,256]{2,1,0:T(8,128)}, u32[]{:S(2)}) copy-start(f32[16,256,256]{2,1,0:T(8,128)} %get-tuple-element.32) | copy-start | bytes 12582916
  66.5 11.1 %collective-permute-start.5 = (bf16[1,256,2048]{2,1,0:T(8,128)(2,1)}, bf16[1,256,2048]{2,1,0:T(8,128)(2,1)}, u32[]{:S(2)}, u32[]{:S(2)}) collective-permute-start(bf16[1,256,2048]{2,1,0:T(8,128)(2,1)} %collective-permute-done.3), channel_id=1, source_target_pairs={{0,64},{64,0},{128,192},{192,128},{1,65},{65,1},{129,193},{193,129... | collective-permute-start | bytes 3145736 | tf_op jit(solution)/shard_map/ppermute | solution.py:17
  66.8 6.3 %copy-start.1 = (f32[16,256,256]{2,1,0:T(8,128)S(1)}, f32[16,256,256]{2,1,0:T(8,128)}, u32[]{:S(2)}) copy-start(f32[16,256,256]{2,1,0:T(8,128)} %get-tuple-element.28) | copy-start | bytes 12582916
  66.8 6.3 %copy-start.3 = (bf16[1,256,2048]{1,2,0:T(8,128)(2,1)S(1)}, bf16[1,256,2048]{1,2,0:T(8,128)(2,1)}, u32[]{:S(2)}) copy-start(bf16[1,256,2048]{1,2,0:T(8,128)(2,1)} %copy.61) | copy-start | bytes 3145732
  84.9 2.0 copy-start.6
  86.9 1.4 copy-start.9
  98.0 89.9 %all-to-all-start = ((bf16[64,80,256]{2,1,0:T(8,128)(2,1)}), bf16[64,80,256]{2,1,0:T(8,128)(2,1)S(1)}, u32[]{:S(2)}, u32[]{:S(2)}) async-start(bf16[64,80,256]{2,1,0:T(8,128)(2,1)} %reshape.341), calls=%async_computation | async-start | bytes 5242880 | tf_op jit(solution)/shard_map/all_to_all | solution.py:99
  115.3 72.7 %collective-permute-start.7 = (bf16[2048,512]{1,0:T(8,128)(2,1)}, bf16[2048,512]{1,0:T(8,128)(2,1)}, u32[]{:S(2)}, u32[]{:S(2)}) collective-permute-start(bf16[2048,512]{1,0:T(8,128)(2,1)} %bitcast.52), channel_id=1, source_target_pairs={{0,128},{64,192},{128,0},{192,64},{1,129},{65,193},{129,1},{193,65... | collective-permute-start | bytes 6291464 | tf_op jit(solution)/shard_map/ppermute | solution.py:12
  116.8 83.6 %collective-permute-start.8 = (bf16[2048,512]{1,0:T(8,128)(2,1)}, bf16[2048,512]{1,0:T(8,128)(2,1)}, u32[]{:S(2)}, u32[]{:S(2)}) collective-permute-start(bf16[2048,512]{1,0:T(8,128)(2,1)} %bitcast.52), channel_id=1, source_target_pairs={{0,64},{64,0},{128,192},{192,128},{1,65},{65,1},{129,193},{193,129... | collective-permute-start | bytes 6291464 | tf_op jit(solution)/shard_map/ppermute | solution.py:17
  116.8 88.8 %collective-permute-start.9 = (bf16[256,2048]{1,0:T(8,128)(2,1)}, bf16[256,2048]{1,0:T(8,128)(2,1)}, u32[]{:S(2)}, u32[]{:S(2)}) collective-permute-start(bf16[256,2048]{1,0:T(8,128)(2,1)} %bitcast.30), channel_id=1, source_target_pairs={{0,64},{64,0},{128,192},{192,128},{1,65},{65,1},{129,193},{193,129... | collective-permute-start | bytes 3145736 | tf_op jit(solution)/shard_map/ppermute | solution.py:17
  117.3 93.5 %collective-permute-start.11 = (bf16[256,2048]{1,0:T(8,128)(2,1)}, bf16[256,2048]{1,0:T(8,128)(2,1)}, u32[]{:S(2)}, u32[]{:S(2)}) collective-permute-start(bf16[256,2048]{1,0:T(8,128)(2,1)} %collective-permute-done.6), channel_id=1, source_target_pairs={{0,64},{64,0},{128,192},{192,128},{1,65},{65,1},{129,193},{193,129... | collective-permute-start | bytes 3145736 | tf_op jit(solution)/shard_map/ppermute | solution.py:17
  187.9 19.8 %collective-permute-start.10 = (bf16[2048,512]{1,0:T(8,128)(2,1)}, bf16[2048,512]{1,0:T(8,128)(2,1)}, u32[]{:S(2)}, u32[]{:S(2)}) collective-permute-start(bf16[2048,512]{1,0:T(8,128)(2,1)} %collective-permute-done.7), channel_id=1, source_target_pairs={{0,64},{64,0},{128,192},{192,128},{1,65},{65,1},{129,193},{193,129... | collective-permute-start | bytes 6291464 | tf_op jit(solution)/shard_map/ppermute | solution.py:17
  191.1 4.0 %copy-start.5 = (bf16[640,2048]{1,0:T(8,128)(2,1)S(1)}, bf16[640,2048]{1,0:T(8,128)(2,1)}, u32[]{:S(2)}) copy-start(bf16[640,2048]{1,0:T(8,128)(2,1)} %reshape.342) | copy-start | bytes 7864324
  216.7 11.7 %copy-start.10 = (f32[1,256,2]{1,2,0:T(2,128)S(1)}, f32[1,256,2]{1,2,0:T(2,128)}, u32[]{:S(2)}) copy-start(f32[1,256,2]{1,2,0:T(2,128)} %param.15) | copy-start | bytes 6148
  216.7 74.6 %all-to-all-start.1 = ((bf16[64,80,256]{2,1,0:T(8,128)(2,1)}), bf16[64,80,256]{2,1,0:T(8,128)(2,1)}, u32[]{:S(2)}, u32[]{:S(2)}) async-start(bf16[64,80,256]{2,1,0:T(8,128)(2,1)} %reshape.343), calls=%async_computation.1 | async-start | bytes 5242880 | tf_op jit(solution)/shard_map/all_to_all | solution.py:111
  (1 other events, 1.0 us)

commit v2 on v0

--- a/solution.py
+++ b/solution.py
@@ -91,9 +91,9 @@
         .at[destination]
         .set(jnp.arange(token_count * top_count, dtype=jnp.int32) // top_count)
     )
-    normed, gate_up_far = lax.optimization_barrier((normed, gate_up_far))
     send_buffer = normed.reshape(token_count, feature_count)[slot_token]
     send_buffer = send_buffer.reshape(expert_count, capacity * 8, feature_count // 8)
+    send_buffer, gate_up_far = lax.optimization_barrier((send_buffer, gate_up_far))
     gate_up_blocks = near_blocks(gate_up_local, gate_up_far)
     down_blocks = near_blocks(down_local, down_far)
     portion = lax.all_to_all(send_buffer, "exp", split_axis=0, concat_axis=0, tiled=True)

time: 300 us -> 291 us (0.970)
  waiting for transfers between devices: 167 us -> 157 us
    ppermute x4, waiting for transfers between devices: 91 us -> 80.1 us  [far_block(): return lax.ppermute(block, 'ctx', perm=[(c, c ^ 2) for c in range(4)])]
    unnamed x33 -> x31, local copies, waits for them, and re-layouts: 8.98 us -> 10.4 us
  transfers between devices with their start and end apart: 14 -> 14, of which waited for: 6 -> 6; matrix products, arithmetic and copies ran while one was open for 25% -> 30% of each run, Pallas kernels for 0% -> 0%
where the time goes in v2:
time: 291 us; the launch traced here: 290 us
  waiting for transfers between devices  157 us (54%)
  matrix products  49.8 us (17%)
  local copies, waits for them, and re-layouts  46.5 us (16%)
  starting transfers between devices  24.2 us (8%)
  other arithmetic  12 us (4%)
    ppermute x4, waiting for transfers between devices, far_block(): return lax.ppermute(block, 'ctx', perm=[(c, c ^ 2) for c in range(4)])  80.1 us
    all_to_all x1, waiting for transfers between devices, shards(): lax.all_to_all(summed, 'exp', split_axis=0, concat_axis=0, tiled=True)  60.8 us
    all_to_all x1, waiting for transfers between devices, shards(): lax.all_to_all(send_buffer, 'exp', split_axis=0, concat_axis=0, tiled=True)  15.7 us
    dot_general x4, matrix products, shards(): jnp.einsum('cqhd,ckhd->cqhk', query_heads, block.reshape(clip_count, -1,...  14.7 us
    dot_general x4, matrix products, shards(): jnp.einsum('cqhk,ckhd->cqhd', expo.astype(jnp.bfloat16), block.reshape(cl...  13.9 us
    dot_general x4, matrix products, shards(): jnp.dot(flattened, gate_up_block, preferred_element_type=jnp.float32)  13.4 us
    all_to_all x1, starting transfers between devices, shards(): lax.all_to_all(send_buffer, 'exp', split_axis=0, concat_axis=0, tiled=True)  12.7 us
    unnamed x31, local copies, waits for them, and re-layouts  10.4 us
  transfers between devices with their start and end apart: 14, of which 6 were waited for; matrix products, arithmetic and copies ran while one was open for 30% of the time, Pallas kernels for 0%

profile of v2, /device:TPU:4, one launch (start us, length us, event | category | flops | bytes accessed | tf_op | source)
XLA Modules:
  0.0 289.6 jit_solution(7420267884509276519)
XLA Ops:
  11.9 3.5 %copy.81 = bf16[256,8,2,256]{3,1,2,0:T(8,128)(2,1)} copy(bf16[256,8,2,256]{3,2,1,0:T(2,128)(2,1)} %bitcast.165) | data formatting | bytes 4194304
  18.0 11.0 %collective-permute-done = bf16[1,256,2048]{1,2,0:T(8,128)(2,1)} collective-permute-done((bf16[1,256,2048]{1,2,0:T(8,128)(2,1)}, bf16[1,256,2048]{1,2,0:T(8,128)(2,1)}, u32[]{:S(2)}, u32[]{:S(2)}) %collective-permute-start) | collective-permute-done | bytes 1048608 | tf_op jit(solution)/shard_map/ppermute | solution.py:12
  34.3 4.0 %bitcast_reduce_fusion.2 = (f32[256,16]{0,1:T(8,128)S(1)}, f32[16,256,256]{2,1,0:T(8,128)}) fusion(bf16[256,16,128]{0,2,1:T(8,128)(2,1)} %bitcast.3, bf16[256,16,128]{2,1,0:T(8,128)(2,1)S(1)} %bitcast.155), kind=kOutput, calls=%fused_computation.12 | convolution fusion | flops 270528512 | bytes 6307840 | tf_op jit(solution)/shard_map/cqhd,ckhd->cqhk/dot_general | solution.py:47
  38.3 4.0 %bitcast_reduce_fusion.1 = (f32[256,16]{0,1:T(8,128)S(1)}, f32[16,256,256]{2,1,0:T(8,128)}) fusion(bf16[256,16,128]{0,2,1:T(8,128)(2,1)} %bitcast.6, bf16[256,16,128]{2,1,0:T(8,128)(2,1)S(1)} %bitcast.156), kind=kOutput, calls=%fused_computation.9 | convolution fusion | flops 270528512 | bytes 6307840 | tf_op jit(solution)/shard_map/cqhd,ckhd->cqhk/dot_general | solution.py:47
  42.3 4.0 %bitcast_reduce_fusion = (f32[256,16]{0,1:T(8,128)S(1)}, f32[16,256,256]{2,1,0:T(8,128)}) fusion(bf16[256,16,128]{0,2,1:T(8,128)(2,1)} %bitcast.9, bf16[256,16,128]{2,1,0:T(8,128)(2,1)S(1)} %bitcast.157), kind=kOutput, calls=%fused_computation.6 | convolution fusion | flops 270528512 | bytes 6307840 | tf_op jit(solution)/shard_map/cqhd,ckhd->cqhk/dot_general | solution.py:47
  46.3 12.8 %collective-permute-done.3 = bf16[1,256,2048]{2,1,0:T(8,128)(2,1)S(1)} collective-permute-done((bf16[1,256,2048]{2,1,0:T(8,128)(2,1)}, bf16[1,256,2048]{2,1,0:T(8,128)(2,1)S(1)}, u32[]{:S(2)}, u32[]{:S(2)}) %collective-permute-start.3) | collective-permute-done | bytes 1048608 | tf_op jit(solution)/shard_map/ppermute | solution.py:12
  60.7 3.6 %fusion.23 = f32[16,128,256]{2,1,0:T(8,128)S(1)} fusion(bf16[256,16,128]{0,2,1:T(8,128)(2,1)} %bitcast.161, f32[16,256,256]{2,1,0:T(8,128)} %get-tuple-element.30, f32[256,16]{0,1:T(8,128)S(1)} %maximum_maximum_fusion), kind=kOutput, calls=%fused_computation.41 | convolution fusion | flops 271581184 | bytes 7356416 | tf_op jit(solution)/shard_map/cqhk,ckhd->cqhd/dot_general | solution.py:64
  64.7 6.2 %fusion.6 = (f32[256,16]{0,1:T(8,128)S(1)}, f32[256,16]{0,1:T(8,128)S(1)}, f32[256,16]{0,1:T(8,128)S(1)}, f32[256,16]{0,1:T(8,128)S(1)}) fusion(f32[16,256,256]{2,1,0:T(8,128)} %get-tuple-element.30, f32[256,16]{0,1:T(8,128)S(1)} %maximum_maximum_fusion, f32[16,256,256]{2,1,0:T(8,128)S(1)} %copy-done, f32[16,256,256]{2,1,0:T(8,128)} %get-tuple-element.28, ...), kind=kLoop, calls=%fused_computation.19 | loop fusion | flops 12566528 | bytes 16859136 | tf_op jit(solution)/shard_map/reduce_sum | solution.py:63
  77.0 5.9 %bitcast_divide_fusion = f32[1,256,16,128]{1,3,2,0:T(8,128)} fusion(f32[16,256,128]{1,2,0:T(8,128)} %fusion.20, f32[16,128,256]{2,1,0:T(8,128)S(1)} %fusion.23, f32[16,256,128]{1,2,0:T(8,128)} %fusion.26, f32[256,16]{0,1:T(8,128)S(1)} %add_add_fusion, bf16[256,16,128]{0,2,1:T(8,128)(2,1)S(1)} %bitcast.164, f32[16,256,256]{2,1,0:T(8,128)} %get-tuple-element.26, ...), kind=kOutput, calls=%fused_computation.47 | convolution fusion | flops 273678336 | bytes 13664256 | tf_op jit(solution)/shard_map/cqhk,ckhd->cqhd/dot_general | solution.py:64
  86.6 4.1 %gather_fusion = bf16[640,2048]{1,0:T(8,128)(2,1)} fusion(bf16[256,2048]{1,0:T(8,128)(2,1)S(1)} %fusion.38, s32[1024]{0:T(1024)S(1)} %pad_clamp_fusion.2), kind=kCustom, calls=%fused_computation | custom fusion | bytes 5245440 | tf_op jit(solution)/shard_map/gather | solution.py:94
  90.7 5.3 %reshape.341 = bf16[64,80,256]{2,1,0:T(8,128)(2,1)} reshape(bf16[640,2048]{1,0:T(8,128)(2,1)} %gather_fusion) | data formatting | bytes 5242880 | tf_op jit(solution)/shard_map/reshape | solution.py:95
  95.9 12.1 %collective-permute-done.6 = bf16[2048,512]{1,0:T(8,128)(2,1)} collective-permute-done((bf16[2048,512]{1,0:T(8,128)(2,1)}, bf16[2048,512]{1,0:T(8,128)(2,1)}, u32[]{:S(2)}, u32[]{:S(2)}) %collective-permute-start.6) | collective-permute-done | bytes 2097184 | tf_op jit(solution)/shard_map/ppermute | solution.py:12
  108.0 12.7 %all-to-all-start = ((bf16[64,80,256]{2,1,0:T(8,128)(2,1)}), bf16[64,80,256]{2,1,0:T(8,128)(2,1)S(1)}, u32[]{:S(2)}, u32[]{:S(2)}) async-start(bf16[64,80,256]{2,1,0:T(8,128)(2,1)} %reshape.341), calls=%async_computation | async-start | bytes 5242880 | tf_op jit(solution)/shard_map/all_to_all | solution.py:99
  122.2 44.3 %collective-permute-done.7 = bf16[256,2048]{1,0:T(8,128)(2,1)} collective-permute-done((bf16[256,2048]{1,0:T(8,128)(2,1)}, bf16[256,2048]{1,0:T(8,128)(2,1)}, u32[]{:S(2)}, u32[]{:S(2)}) %collective-permute-start.7) | collective-permute-done | bytes 1048608 | tf_op jit(solution)/shard_map/ppermute | solution.py:12
  166.5 15.7 %all-to-all-done = bf16[64,80,256]{2,1,0:T(8,128)(2,1)S(1)} async-done(((bf16[64,80,256]{2,1,0:T(8,128)(2,1)}), bf16[64,80,256]{2,1,0:T(8,128)(2,1)S(1)}, u32[]{:S(2)}, u32[]{:S(2)}) %all-to-all-start) | async-done | bytes 2621472 | tf_op jit(solution)/shard_map/all_to_all | solution.py:99
  182.2 3.1 %reshape.342 = bf16[640,2048]{1,0:T(8,128)(2,1)} reshape(bf16[64,80,256]{2,1,0:T(8,128)(2,1)S(1)} %all-to-all-done) | data formatting | bytes 5242880 | tf_op jit(solution)/shard_map/reshape | solution.py:100
  185.3 4.0 %fusion.83 = f32[640,512]{1,0:T(8,128)S(1)} fusion(bf16[640,2048]{1,0:T(8,128)(2,1)} %reshape.342, bf16[2048,512]{1,0:T(8,128)(2,1)} %collective-permute-done.6), kind=kOutput, calls=%fused_computation.125 | convolution fusion | flops 1342177280 | bytes 6029312 | tf_op jit(solution)/shard_map/dot_general | solution.py:103
  189.4 3.2 %fusion.82 = f32[640,512]{1,0:T(8,128)S(1)} fusion(bf16[640,2048]{1,0:T(8,128)(2,1)S(1)} %copy-done.6, bf16[2048,512]{1,0:T(8,128)(2,1)} %bitcast.52), kind=kOutput, calls=%fused_computation.124 | convolution fusion | flops 1342177280 | bytes 6029312 | tf_op jit(solution)/shard_map/dot_general | solution.py:103
  193.5 3.1 %fusion.84 = f32[640,512]{1,0:T(8,128)S(1)} fusion(bf16[640,2048]{1,0:T(8,128)(2,1)S(1)} %copy-done.6, bf16[2048,512]{1,0:T(8,128)(2,1)} %collective-permute-done.8), kind=kOutput, calls=%fused_computation.126 | convolution fusion | flops 1342177280 | bytes 6029312 | tf_op jit(solution)/shard_map/dot_general | solution.py:103
  206.6 3.2 %reshape.343 = bf16[64,80,256]{2,1,0:T(8,128)(2,1)} reshape(bf16[640,2048]{1,0:T(8,128)(2,1)S(1)} %add_convert_fusion) | data formatting | bytes 5242880 | tf_op jit(solution)/shard_map/reshape | solution.py:110
  209.8 6.5 %all-to-all-start.1 = ((bf16[64,80,256]{2,1,0:T(8,128)(2,1)}), bf16[64,80,256]{2,1,0:T(8,128)(2,1)}, u32[]{:S(2)}, u32[]{:S(2)}) async-start(bf16[64,80,256]{2,1,0:T(8,128)(2,1)} %reshape.343), calls=%async_computation.1 | async-start | bytes 5242880 | tf_op jit(solution)/shard_map/all_to_all | solution.py:111
  216.7 60.8 %all-to-all-done.1 = bf16[64,80,256]{2,1,0:T(8,128)(2,1)} async-done(((bf16[64,80,256]{2,1,0:T(8,128)(2,1)}), bf16[64,80,256]{2,1,0:T(8,128)(2,1)}, u32[]{:S(2)}, u32[]{:S(2)}) %all-to-all-start.1) | async-done | bytes 2621472 | tf_op jit(solution)/shard_map/all_to_all | solution.py:111
  277.6 3.9 %reshape.344 = bf16[640,2048]{1,0:T(8,128)(2,1)S(1)} reshape(bf16[64,80,256]{2,1,0:T(8,128)(2,1)} %all-to-all-done.1) | data formatting | bytes 5242880 | tf_op jit(solution)/shard_map/reshape | solution.py:112
  286.2 3.4 %fusion.15 = bf16[1,256,2048]{2,1,0:T(8,128)(2,1)} fusion(bf16[1,256,2048]{2,1,0:T(8,128)(2,1)} %copy-done.2, bf16[256,2048]{1,0:T(8,128)(2,1)} %gather_fusion.2, bf16[256,2048]{1,0:T(8,128)(2,1)} %gather_fusion.1, f32[256]{0:T(256)S(1)} %bitcast.169, f32[256]{0:T(256)S(1)} %bitcast.168), kind=kLoop, calls=%fused_computation.35 | loop fusion | flops 4194304 | bytes 4196352 | tf_op jit(solution)/shard_map/convert_element_type | solution.py:119
  (91 shorter events, 48.9 us)
Async XLA Ops:
  2.3 26.7 %collective-permute-start = (bf16[1,256,2048]{1,2,0:T(8,128)(2,1)}, bf16[1,256,2048]{1,2,0:T(8,128)(2,1)}, u32[]{:S(2)}, u32[]{:S(2)}) collective-permute-start(bf16[1,256,2048]{1,2,0:T(8,128)(2,1)} %copy.49), channel_id=1, source_target_pairs={{0,128},{64,192},{128,0},{192,64},{1,129},{65,193},{129,1},{193,65... | collective-permute-start | bytes 3145736 | tf_op jit(solution)/shard_map/ppermute | solution.py:12
  4.5 33.8 %collective-permute-start.1 = (bf16[1,256,2048]{1,2,0:T(8,128)(2,1)}, bf16[1,256,2048]{1,2,0:T(8,128)(2,1)}, u32[]{:S(2)}, u32[]{:S(2)}) collective-permute-start(bf16[1,256,2048]{1,2,0:T(8,128)(2,1)} %copy.49), channel_id=1, source_target_pairs={{0,64},{64,0},{128,192},{192,128},{1,65},{65,1},{129,193},{193,129... | collective-permute-start | bytes 3145736 | tf_op jit(solution)/shard_map/ppermute | solution.py:17
  4.5 27.5 %collective-permute-start.4 = (bf16[1,256,2048]{2,1,0:T(8,128)(2,1)}, bf16[1,256,2048]{2,1,0:T(8,128)(2,1)}, u32[]{:S(2)}, u32[]{:S(2)}) collective-permute-start(bf16[1,256,2048]{2,1,0:T(8,128)(2,1)} %param.11), channel_id=1, source_target_pairs={{0,64},{64,0},{128,192},{192,128},{1,65},{65,1},{129,193},{193,129... | collective-permute-start | bytes 3145736 | tf_op jit(solution)/shard_map/ppermute | solution.py:17
  5.8 4.7 %copy-start.4 = (bf16[1,256,2048]{2,1,0:T(8,128)(2,1)S(1)}, bf16[1,256,2048]{2,1,0:T(8,128)(2,1)}, u32[]{:S(2)}) copy-start(bf16[1,256,2048]{2,1,0:T(8,128)(2,1)} %param.10) | copy-start | bytes 3145732
  11.8 17.2 %copy-start.5 = (bf16[32,8,16,128]{3,2,1,0:T(8,128)(2,1)S(1)}, bf16[32,8,16,128]{3,2,1,0:T(8,128)(2,1)}, u32[]{:S(2)}) copy-start(bf16[32,8,16,128]{3,2,1,0:T(8,128)(2,1)} %copy.79) | copy-start | bytes 3145732
  29.0 13.3 %collective-permute-start.2 = (bf16[1,256,2048]{1,2,0:T(8,128)(2,1)}, bf16[1,256,2048]{1,2,0:T(8,128)(2,1)}, u32[]{:S(2)}, u32[]{:S(2)}) collective-permute-start(bf16[1,256,2048]{1,2,0:T(8,128)(2,1)} %collective-permute-done), channel_id=1, source_target_pairs={{0,64},{64,0},{128,192},{192,128},{1,65},{65,1},{129,193},{193,129... | collective-permute-start | bytes 3145736 | tf_op jit(solution)/shard_map/ppermute | solution.py:17
  31.7 27.3 %collective-permute-start.3 = (bf16[1,256,2048]{2,1,0:T(8,128)(2,1)}, bf16[1,256,2048]{2,1,0:T(8,128)(2,1)S(1)}, u32[]{:S(2)}, u32[]{:S(2)}) collective-permute-start(bf16[1,256,2048]{2,1,0:T(8,128)(2,1)} %param.11), channel_id=1, source_target_pairs={{0,128},{64,192},{128,0},{192,64},{1,129},{65,193},{129,1},{193,65... | collective-permute-start | bytes 3145736 | tf_op jit(solution)/shard_map/ppermute | solution.py:12
  59.0 49.0 %collective-permute-start.6 = (bf16[2048,512]{1,0:T(8,128)(2,1)}, bf16[2048,512]{1,0:T(8,128)(2,1)}, u32[]{:S(2)}, u32[]{:S(2)}) collective-permute-start(bf16[2048,512]{1,0:T(8,128)(2,1)} %bitcast.52), channel_id=1, source_target_pairs={{0,128},{64,192},{128,0},{192,64},{1,129},{65,193},{129,1},{193,65... | collective-permute-start | bytes 6291464 | tf_op jit(solution)/shard_map/ppermute | solution.py:12
  60.7 3.6 %copy-start.9 = (bf16[1,256,2048]{2,1,0:T(8,128)(2,1)S(1)}, bf16[1,256,2048]{2,1,0:T(8,128)(2,1)}, u32[]{:S(2)}) copy-start(bf16[1,256,2048]{2,1,0:T(8,128)(2,1)} %copy-done.8) | copy-start | bytes 3145732
  60.7 4.1 %copy-start = (f32[16,256,256]{2,1,0:T(8,128)S(1)}, f32[16,256,256]{2,1,0:T(8,128)}, u32[]{:S(2)}) copy-start(f32[16,256,256]{2,1,0:T(8,128)} %get-tuple-element.32) | copy-start | bytes 12582916
  64.2 11.3 %collective-permute-start.5 = (bf16[1,256,2048]{2,1,0:T(8,128)(2,1)S(1)}, bf16[1,256,2048]{2,1,0:T(8,128)(2,1)}, u32[]{:S(2)}, u32[]{:S(2)}) collective-permute-start(bf16[1,256,2048]{2,1,0:T(8,128)(2,1)S(1)} %copy-done.9), channel_id=1, source_target_pairs={{0,64},{64,0},{128,192},{192,128},{1,65},{65,1},{129,193},{193,129... | collective-permute-start | bytes 3145736 | tf_op jit(solution)/shard_map/ppermute | solution.py:17
  64.7 6.2 %copy-start.1 = (f32[16,256,256]{2,1,0:T(8,128)S(1)}, f32[16,256,256]{2,1,0:T(8,128)}, u32[]{:S(2)}) copy-start(f32[16,256,256]{2,1,0:T(8,128)} %get-tuple-element.28) | copy-start | bytes 12582916
  64.7 6.3 %copy-start.3 = (bf16[1,256,2048]{1,2,0:T(8,128)(2,1)S(1)}, bf16[1,256,2048]{1,2,0:T(8,128)(2,1)}, u32[]{:S(2)}) copy-start(bf16[1,256,2048]{1,2,0:T(8,128)(2,1)} %copy.61) | copy-start | bytes 3145732
  82.9 2.0 copy-start.7
  108.0 74.1 %all-to-all-start = ((bf16[64,80,256]{2,1,0:T(8,128)(2,1)}), bf16[64,80,256]{2,1,0:T(8,128)(2,1)S(1)}, u32[]{:S(2)}, u32[]{:S(2)}) async-start(bf16[64,80,256]{2,1,0:T(8,128)(2,1)} %reshape.341), calls=%async_computation | async-start | bytes 5242880 | tf_op jit(solution)/shard_map/all_to_all | solution.py:99
  120.8 45.7 %collective-permute-start.7 = (bf16[256,2048]{1,0:T(8,128)(2,1)}, bf16[256,2048]{1,0:T(8,128)(2,1)}, u32[]{:S(2)}, u32[]{:S(2)}) collective-permute-start(bf16[256,2048]{1,0:T(8,128)(2,1)} %bitcast.172), channel_id=1, source_target_pairs={{0,128},{64,192},{128,0},{192,64},{1,129},{65,193},{129,1},{193,65... | collective-permute-start | bytes 3145736 | tf_op jit(solution)/shard_map/ppermute | solution.py:12
  121.7 71.8 %collective-permute-start.8 = (bf16[2048,512]{1,0:T(8,128)(2,1)}, bf16[2048,512]{1,0:T(8,128)(2,1)}, u32[]{:S(2)}, u32[]{:S(2)}) collective-permute-start(bf16[2048,512]{1,0:T(8,128)(2,1)} %bitcast.52), channel_id=1, source_target_pairs={{0,64},{64,0},{128,192},{192,128},{1,65},{65,1},{129,193},{193,129... | collective-permute-start | bytes 6291464 | tf_op jit(solution)/shard_map/ppermute | solution.py:17
  121.7 77.0 %collective-permute-start.9 = (bf16[256,2048]{1,0:T(8,128)(2,1)}, bf16[256,2048]{1,0:T(8,128)(2,1)}, u32[]{:S(2)}, u32[]{:S(2)}) collective-permute-start(bf16[256,2048]{1,0:T(8,128)(2,1)} %bitcast.173), channel_id=1, source_target_pairs={{0,64},{64,0},{128,192},{192,128},{1,65},{65,1},{129,193},{193,129... | collective-permute-start | bytes 3145736 | tf_op jit(solution)/shard_map/ppermute | solution.py:17
  122.2 78.6 %collective-permute-start.10 = (bf16[2048,512]{1,0:T(8,128)(2,1)}, bf16[2048,512]{1,0:T(8,128)(2,1)}, u32[]{:S(2)}, u32[]{:S(2)}) collective-permute-start(bf16[2048,512]{1,0:T(8,128)(2,1)} %collective-permute-done.6), channel_id=1, source_target_pairs={{0,64},{64,0},{128,192},{192,128},{1,65},{65,1},{129,193},{193,129... | collective-permute-start | bytes 6291464 | tf_op jit(solution)/shard_map/ppermute | solution.py:17
  166.5 37.4 %collective-permute-start.11 = (bf16[256,2048]{1,0:T(8,128)(2,1)}, bf16[256,2048]{1,0:T(8,128)(2,1)}, u32[]{:S(2)}, u32[]{:S(2)}) collective-permute-start(bf16[256,2048]{1,0:T(8,128)(2,1)} %collective-permute-done.7), channel_id=1, source_target_pairs={{0,64},{64,0},{128,192},{192,128},{1,65},{65,1},{129,193},{193,129... | collective-permute-start | bytes 3145736 | tf_op jit(solution)/shard_map/ppermute | solution.py:17
  185.3 4.0 %copy-start.6 = (bf16[640,2048]{1,0:T(8,128)(2,1)S(1)}, bf16[640,2048]{1,0:T(8,128)(2,1)}, u32[]{:S(2)}) copy-start(bf16[640,2048]{1,0:T(8,128)(2,1)} %reshape.342) | copy-start | bytes 7864324
  189.4 3.2 %copy-start.12 = (bf16[1,256,2048]{2,1,0:T(8,128)(2,1)S(1)}, bf16[1,256,2048]{2,1,0:T(8,128)(2,1)}, u32[]{:S(2)}) copy-start(bf16[1,256,2048]{2,1,0:T(8,128)(2,1)} %param.17) | copy-start | bytes 3145732
  209.8 6.9 %copy-start.11 = (f32[1,256,2]{1,2,0:T(2,128)S(1)}, f32[1,256,2]{1,2,0:T(2,128)}, u32[]{:S(2)}) copy-start(f32[1,256,2]{1,2,0:T(2,128)} %param.15) | copy-start | bytes 6148
  209.8 67.8 %all-to-all-start.1 = ((bf16[64,80,256]{2,1,0:T(8,128)(2,1)}), bf16[64,80,256]{2,1,0:T(8,128)(2,1)}, u32[]{:S(2)}, u32[]{:S(2)}) async-start(bf16[64,80,256]{2,1,0:T(8,128)(2,1)} %reshape.343), calls=%async_computation.1 | async-start | bytes 5242880 | tf_op jit(solution)/shard_map/all_to_all | solution.py:111
  (3 other events, 4.0 us)

commit v3 on v2

--- a/solution.py
+++ b/solution.py
@@ -98,13 +98,14 @@
     down_blocks = near_blocks(down_local, down_far)
     portion = lax.all_to_all(send_buffer, "exp", split_axis=0, concat_axis=0, tiled=True)
     flattened = portion.reshape(-1, feature_count)
+    block_count = len(gate_up_blocks)
+    gate_and_up = jnp.dot(
+        flattened, jnp.concatenate(gate_up_blocks, axis=1), preferred_element_type=jnp.float32
+    ).reshape(-1, block_count, 2, local_units)
+    hidden = (jax.nn.silu(gate_and_up[:, :, 0]) * gate_and_up[:, :, 1]).astype(jnp.bfloat16)
     summed = None
-    for gate_up_block, down_block in zip(gate_up_blocks, down_blocks):
-        gate_and_up = jnp.dot(flattened, gate_up_block, preferred_element_type=jnp.float32)
-        hidden = (
-            jax.nn.silu(gate_and_up[:, :local_units]) * gate_and_up[:, local_units:]
-        ).astype(jnp.bfloat16)
-        group_part = jnp.dot(hidden, down_block, preferred_element_type=jnp.float32)
+    for index, down_block in enumerate(down_blocks):
+        group_part = jnp.dot(hidden[:, index], down_block, preferred_element_type=jnp.float32)
         group_part = group_part.astype(jnp.bfloat16).astype(jnp.float32)
         summed = group_part if summed is None else summed + group_part
     summed = summed.astype(jnp.bfloat16).reshape(portion.shape)

time: 291 us -> 292 us (level)
  waiting for transfers between devices: 157 us -> 146 us
  other arithmetic: 12 us -> 20.5 us
  local copies, waits for them, and re-layouts: 46.5 us -> 51.4 us
    all_to_all x1, waiting for transfers between devices: 15.7 us -> 6.97 us  [shards(): lax.all_to_all(send_buffer, 'exp', split_axis=0, concat_axis=0, tiled=True)]
    concatenate x0 -> x1, other arithmetic: none -> 6.08 us  [shards(): jnp.concatenate(gate_up_blocks, axis=1)]
    dot_general x8 -> x5, matrix products: 21.2 us -> 16.8 us  [the longest x4 8.74 us: shards(): jnp.dot(hidden[:, index], down_block, preferred_element_type=jnp.float32)]
    another operation x2 -> x3, local copies, waits for them, and re-layouts: 1.49 us -> 4.77 us  [the longest x1 2.47 us: shards(): gate_up_local = gate_up_weight[0].reshape(feature_count, 2 * local_units)]
    unnamed x31 -> x25, local copies, waits for them, and re-layouts: 10.4 us -> 7.64 us
  transfers between devices with their start and end apart: 14 -> 14, of which waited for: 6 -> 6; matrix products, arithmetic and copies ran while one was open for 30% -> 33% of each run, Pallas kernels for 0% -> 0%
where the time goes in v3:
time: 292 us; the launch traced here: 291 us
  waiting for transfers between devices  146 us (50%)
  local copies, waits for them, and re-layouts  51.4 us (18%)
  matrix products  48.3 us (17%)
  starting transfers between devices  24.1 us (8%)
  other arithmetic  20.5 us (7%)
    ppermute x4, waiting for transfers between devices, far_block(): return lax.ppermute(block, 'ctx', perm=[(c, c ^ 2) for c in range(4)])  78.3 us
    all_to_all x1, waiting for transfers between devices, shards(): lax.all_to_all(summed, 'exp', split_axis=0, concat_axis=0, tiled=True)  60.8 us
    dot_general x4, matrix products, shards(): jnp.einsum('cqhd,ckhd->cqhk', query_heads, block.reshape(clip_count, -1,...  15.9 us
    dot_general x4, matrix products, shards(): jnp.einsum('cqhk,ckhd->cqhd', expo.astype(jnp.bfloat16), block.reshape(cl...  15.5 us
    all_to_all x1, starting transfers between devices, shards(): lax.all_to_all(send_buffer, 'exp', split_axis=0, concat_axis=0, tiled=True)  13 us
    dot_general x4, matrix products, shards(): jnp.dot(hidden[:, index], down_block, preferred_element_type=jnp.float32)  8.74 us
    dot_general x1, matrix products, shards(): jnp.dot(flattened, jnp.concatenate(gate_up_blocks, axis=1), preferred_ele...  8.03 us
    unnamed x25, local copies, waits for them, and re-layouts  7.64 us
  transfers between devices with their start and end apart: 14, of which 6 were waited for; matrix products, arithmetic and copies ran while one was open for 33% of the time, Pallas kernels for 0%

profile of v3, /device:TPU:4, one launch (start us, length us, event | category | flops | bytes accessed | tf_op | source)
XLA Modules:
  0.0 290.7 jit_solution(6145487530402140380)
XLA Ops:
  16.3 12.8 %collective-permute-done = bf16[1,256,2048]{1,2,0:T(8,128)(2,1)} collective-permute-done((bf16[1,256,2048]{1,2,0:T(8,128)(2,1)}, bf16[1,256,2048]{1,2,0:T(8,128)(2,1)}, u32[]{:S(2)}, u32[]{:S(2)}) %collective-permute-start) | collective-permute-done | bytes 1048608 | tf_op jit(solution)/shard_map/ppermute | solution.py:12
  29.1 4.0 %bitcast_reduce_fusion.3 = (f32[256,16]{0,1:T(8,128)S(1)}, f32[16,256,256]{2,1,0:T(8,128)}) fusion(bf16[256,16,128]{2,1,0:T(8,128)(2,1)S(1)} %bitcast.177, bf16[256,16,128]{2,1,0:T(8,128)(2,1)} %bitcast.189), kind=kOutput, calls=%fused_computation.16 | convolution fusion | flops 270528512 | bytes 6307840 | tf_op jit(solution)/shard_map/cqhd,ckhd->cqhk/dot_general | solution.py:47
  35.6 4.0 %bitcast_reduce_fusion.2 = (f32[256,16]{0,1:T(8,128)S(1)}, f32[16,256,256]{2,1,0:T(8,128)}) fusion(bf16[256,16,128]{0,2,1:T(8,128)(2,1)} %bitcast.3, bf16[256,16,128]{2,1,0:T(8,128)(2,1)S(1)} %bitcast.178), kind=kOutput, calls=%fused_computation.13 | convolution fusion | flops 270528512 | bytes 6307840 | tf_op jit(solution)/shard_map/cqhd,ckhd->cqhk/dot_general | solution.py:47
  39.6 4.0 %bitcast_reduce_fusion.1 = (f32[256,16]{0,1:T(8,128)S(1)}, f32[16,256,256]{2,1,0:T(8,128)}) fusion(bf16[256,16,128]{0,2,1:T(8,128)(2,1)} %bitcast.6, bf16[256,16,128]{2,1,0:T(8,128)(2,1)S(1)} %bitcast.179), kind=kOutput, calls=%fused_computation.10 | convolution fusion | flops 270528512 | bytes 6307840 | tf_op jit(solution)/shard_map/cqhd,ckhd->cqhk/dot_general | solution.py:47
  43.6 4.0 %bitcast_reduce_fusion = (f32[256,16]{0,1:T(8,128)S(1)}, f32[16,256,256]{2,1,0:T(8,128)}) fusion(bf16[256,16,128]{0,2,1:T(8,128)(2,1)} %bitcast.9, bf16[256,16,128]{2,1,0:T(8,128)(2,1)S(1)} %bitcast.180), kind=kOutput, calls=%fused_computation.7 | convolution fusion | flops 270528512 | bytes 6307840 | tf_op jit(solution)/shard_map/cqhd,ckhd->cqhk/dot_general | solution.py:47
  47.6 12.9 %collective-permute-done.3 = bf16[1,256,2048]{2,1,0:T(8,128)(2,1)} collective-permute-done((bf16[1,256,2048]{2,1,0:T(8,128)(2,1)}, bf16[1,256,2048]{2,1,0:T(8,128)(2,1)}, u32[]{:S(2)}, u32[]{:S(2)}) %collective-permute-start.3) | collective-permute-done | bytes 1048608 | tf_op jit(solution)/shard_map/ppermute | solution.py:12
  64.7 4.6 %fusion.27 = f32[16,128,256]{2,1,0:T(8,128)} fusion(bf16[256,16,128]{0,2,1:T(8,128)(2,1)S(1)} %bitcast.187, f32[16,256,256]{2,1,0:T(8,128)} %get-tuple-element.30, f32[256,16]{0,1:T(8,128)S(1)} %maximum_maximum_fusion), kind=kOutput, calls=%fused_computation.48 | convolution fusion | flops 271581184 | bytes 7356416 | tf_op jit(solution)/shard_map/cqhk,ckhd->cqhd/dot_general | solution.py:64
  69.3 6.2 %fusion.6 = (f32[256,16]{0,1:T(8,128)S(1)}, f32[256,16]{0,1:T(8,128)S(1)}, f32[256,16]{0,1:T(8,128)S(1)}, f32[256,16]{0,1:T(8,128)S(1)}) fusion(f32[16,256,256]{2,1,0:T(8,128)} %get-tuple-element.30, f32[256,16]{0,1:T(8,128)S(1)} %maximum_maximum_fusion, f32[16,256,256]{2,1,0:T(8,128)S(1)} %copy-done, f32[16,256,256]{2,1,0:T(8,128)} %get-tuple-element.28, ...), kind=kLoop, calls=%fused_computation.20 | loop fusion | flops 12566528 | bytes 16859136 | tf_op jit(solution)/shard_map/reduce_sum | solution.py:63
  81.6 6.5 %bitcast_divide_fusion = f32[1,256,16,128]{1,3,2,0:T(8,128)} fusion(f32[16,256,128]{1,2,0:T(8,128)} %fusion.24, f32[16,128,256]{2,1,0:T(8,128)} %fusion.27, f32[16,256,128]{1,2,0:T(8,128)} %fusion.30, f32[256,16]{0,1:T(8,128)S(1)} %add_add_fusion, bf16[256,16,128]{0,2,1:T(8,128)(2,1)S(1)} %bitcast.190, f32[16,256,256]{2,1,0:T(8,128)} %get-tuple-element.26, ...), kind=kOutput, calls=%fused_computation.54 | convolution fusion | flops 273678336 | bytes 13664256 | tf_op jit(solution)/shard_map/cqhk,ckhd->cqhd/dot_general | solution.py:64
  88.0 3.0 %copy.73 = f32[1,256,2048]{2,1,0:T(8,128)} copy(f32[1,256,2048]{1,2,0:T(8,128)} %bitcast.184) | data formatting | bytes 4194304 | tf_op jit(solution)/shard_map/reshape | solution.py:73
  94.4 4.1 %gather_fusion = bf16[640,2048]{1,0:T(8,128)(2,1)} fusion(bf16[256,2048]{1,0:T(8,128)(2,1)S(1)} %fusion.42, s32[1024]{0:T(1024)S(1)} %pad_clamp_fusion.2), kind=kCustom, calls=%fused_computation | custom fusion | bytes 5245440 | tf_op jit(solution)/shard_map/gather | solution.py:94
  98.5 5.3 %reshape.343 = bf16[64,80,256]{2,1,0:T(8,128)(2,1)} reshape(bf16[640,2048]{1,0:T(8,128)(2,1)} %gather_fusion) | data formatting | bytes 5242880 | tf_op jit(solution)/shard_map/reshape | solution.py:95
  103.7 8.2 %collective-permute-done.6 = bf16[2048,512]{0,1:T(8,128)(2,1)} collective-permute-done((bf16[2048,512]{0,1:T(8,128)(2,1)}, bf16[2048,512]{0,1:T(8,128)(2,1)}, u32[]{:S(2)}, u32[]{:S(2)}) %collective-permute-start.6) | collective-permute-done | bytes 2097184 | tf_op jit(solution)/shard_map/ppermute | solution.py:12
  111.9 13.0 %all-to-all-start = ((bf16[64,80,256]{2,1,0:T(8,128)(2,1)}), bf16[64,80,256]{2,1,0:T(8,128)(2,1)}, u32[]{:S(2)}, u32[]{:S(2)}) async-start(bf16[64,80,256]{2,1,0:T(8,128)(2,1)} %reshape.343), calls=%async_computation | async-start | bytes 5242880 | tf_op jit(solution)/shard_map/all_to_all | solution.py:99
  128.7 44.4 %collective-permute-done.9 = bf16[256,2048]{1,0:T(8,128)(2,1)} collective-permute-done((bf16[256,2048]{1,0:T(8,128)(2,1)}, bf16[256,2048]{1,0:T(8,128)(2,1)}, u32[]{:S(2)}, u32[]{:S(2)}) %collective-permute-start.9) | collective-permute-done | bytes 1048608 | tf_op jit(solution)/shard_map/ppermute | solution.py:12
  173.1 6.1 %pad_maximum_fusion = bf16[2048,2048]{0,1:T(8,128)(2,1)} fusion(bf16[2048,512]{0,1:T(8,128)(2,1)S(1)} %collective-permute-done.8, bf16[2048,512]{0,1:T(8,128)(2,1)S(1)} %collective-permute-done.7, bf16[2048,512]{0,1:T(8,128)(2,1)} %collective-permute-done.6, bf16[2048,512]{0,1:T(8,128)(2,1)} %copy.80), kind=kLoop, calls=%fused_computation.4 | loop fusion | flops 33554432 | bytes 16777216 | tf_op jit(solution)/shard_map/concatenate | solution.py:103
  179.2 7.0 %all-to-all-done = bf16[64,80,256]{2,1,0:T(8,128)(2,1)} async-done(((bf16[64,80,256]{2,1,0:T(8,128)(2,1)}), bf16[64,80,256]{2,1,0:T(8,128)(2,1)}, u32[]{:S(2)}, u32[]{:S(2)}) %all-to-all-start) | async-done | bytes 2621472 | tf_op jit(solution)/shard_map/all_to_all | solution.py:99
  186.2 3.9 %reshape.382 = bf16[640,2048,1,1]{1,0,2,3:T(8,128)(2,1)S(1)} reshape(bf16[64,80,256]{2,1,0:T(8,128)(2,1)} %all-to-all-done) | data formatting | bytes 5242880 | tf_op jit(solution)/shard_map/reshape | solution.py:100
  190.1 8.0 %fusion.14 = f32[640,4,2,256]{3,0,2,1:T(8,128)S(1)} fusion(bf16[4,2,256,2048]{3,2,1,0:T(8,128)(2,1)} %bitcast.183, bf16[640,2048,1,1]{1,0,2,3:T(8,128)(2,1)S(1)} %reshape.382), kind=kOutput, calls=%fused_computation.37 | convolution fusion | flops 5368709120 | bytes 16252928 | tf_op jit(solution)/shard_map/dot_general | solution.py:102
  207.7 3.2 %reshape.345 = bf16[64,80,256]{2,1,0:T(8,128)(2,1)} reshape(bf16[640,2048]{1,0:T(8,128)(2,1)S(1)} %add_convert_fusion) | data formatting | bytes 5242880 | tf_op jit(solution)/shard_map/reshape | solution.py:111
  210.9 6.5 %all-to-all-start.1 = ((bf16[64,80,256]{2,1,0:T(8,128)(2,1)}), bf16[64,80,256]{2,1,0:T(8,128)(2,1)}, u32[]{:S(2)}, u32[]{:S(2)}) async-start(bf16[64,80,256]{2,1,0:T(8,128)(2,1)} %reshape.345), calls=%async_computation.1 | async-start | bytes 5242880 | tf_op jit(solution)/shard_map/all_to_all | solution.py:112
  217.9 60.8 %all-to-all-done.1 = bf16[64,80,256]{2,1,0:T(8,128)(2,1)} async-done(((bf16[64,80,256]{2,1,0:T(8,128)(2,1)}), bf16[64,80,256]{2,1,0:T(8,128)(2,1)}, u32[]{:S(2)}, u32[]{:S(2)}) %all-to-all-start.1) | async-done | bytes 2621472 | tf_op jit(solution)/shard_map/all_to_all | solution.py:112
  278.7 3.9 %reshape.346 = bf16[640,2048]{1,0:T(8,128)(2,1)S(1)} reshape(bf16[64,80,256]{2,1,0:T(8,128)(2,1)} %all-to-all-done.1) | data formatting | bytes 5242880 | tf_op jit(solution)/shard_map/reshape | solution.py:113
  287.3 3.4 %fusion.19 = bf16[1,256,2048]{2,1,0:T(8,128)(2,1)} fusion(bf16[1,256,2048]{2,1,0:T(8,128)(2,1)} %copy-done.2, bf16[256,2048]{1,0:T(8,128)(2,1)} %gather_fusion.2, bf16[256,2048]{1,0:T(8,128)(2,1)} %gather_fusion.1, f32[256]{0:T(256)S(1)} %bitcast.195, f32[256]{0:T(256)S(1)} %bitcast.194), kind=kLoop, calls=%fused_computation.42 | loop fusion | flops 4194304 | bytes 4196352 | tf_op jit(solution)/shard_map/convert_element_type | solution.py:120
  (86 shorter events, 50.7 us)
Async XLA Ops:
  0.0 10.0 %copy-start.7 = (bf16[1,256,2048]{2,1,0:T(8,128)(2,1)S(1)}, bf16[1,256,2048]{2,1,0:T(8,128)(2,1)}, u32[]{:S(2)}) copy-start(bf16[1,256,2048]{2,1,0:T(8,128)(2,1)} %param.9) | copy-start | bytes 3145732
  2.4 26.7 %collective-permute-start = (bf16[1,256,2048]{1,2,0:T(8,128)(2,1)}, bf16[1,256,2048]{1,2,0:T(8,128)(2,1)}, u32[]{:S(2)}, u32[]{:S(2)}) collective-permute-start(bf16[1,256,2048]{1,2,0:T(8,128)(2,1)} %copy.57), channel_id=1, source_target_pairs={{0,128},{64,192},{128,0},{192,64},{1,129},{65,193},{129,1},{193,65... | collective-permute-start | bytes 3145736 | tf_op jit(solution)/shard_map/ppermute | solution.py:12
  4.6 35.0 %collective-permute-start.1 = (bf16[1,256,2048]{1,2,0:T(8,128)(2,1)}, bf16[1,256,2048]{1,2,0:T(8,128)(2,1)}, u32[]{:S(2)}, u32[]{:S(2)}) collective-permute-start(bf16[1,256,2048]{1,2,0:T(8,128)(2,1)} %copy.57), channel_id=1, source_target_pairs={{0,64},{64,0},{128,192},{192,128},{1,65},{65,1},{129,193},{193,129... | collective-permute-start | bytes 3145736 | tf_op jit(solution)/shard_map/ppermute | solution.py:17
  4.6 28.8 %collective-permute-start.4 = (bf16[1,256,2048]{2,1,0:T(8,128)(2,1)}, bf16[1,256,2048]{2,1,0:T(8,128)(2,1)}, u32[]{:S(2)}, u32[]{:S(2)}) collective-permute-start(bf16[1,256,2048]{2,1,0:T(8,128)(2,1)} %param.11), channel_id=1, source_target_pairs={{0,64},{64,0},{128,192},{192,128},{1,65},{65,1},{129,193},{193,129... | collective-permute-start | bytes 3145736 | tf_op jit(solution)/shard_map/ppermute | solution.py:17
  5.9 4.3 %copy-start.5 = (bf16[1,256,2048]{2,1,0:T(8,128)(2,1)S(1)}, bf16[1,256,2048]{2,1,0:T(8,128)(2,1)}, u32[]{:S(2)}) copy-start(bf16[1,256,2048]{2,1,0:T(8,128)(2,1)} %param.10) | copy-start | bytes 3145732
  29.1 14.5 %collective-permute-start.2 = (bf16[1,256,2048]{1,2,0:T(8,128)(2,1)}, bf16[1,256,2048]{1,2,0:T(8,128)(2,1)}, u32[]{:S(2)}, u32[]{:S(2)}) collective-permute-start(bf16[1,256,2048]{1,2,0:T(8,128)(2,1)} %collective-permute-done), channel_id=1, source_target_pairs={{0,64},{64,0},{128,192},{192,128},{1,65},{65,1},{129,193},{193,129... | collective-permute-start | bytes 3145736 | tf_op jit(solution)/shard_map/ppermute | solution.py:17
  33.1 27.4 %collective-permute-start.3 = (bf16[1,256,2048]{2,1,0:T(8,128)(2,1)}, bf16[1,256,2048]{2,1,0:T(8,128)(2,1)}, u32[]{:S(2)}, u32[]{:S(2)}) collective-permute-start(bf16[1,256,2048]{2,1,0:T(8,128)(2,1)} %param.11), channel_id=1, source_target_pairs={{0,128},{64,192},{128,0},{192,64},{1,129},{65,193},{129,1},{193,65... | collective-permute-start | bytes 3145736 | tf_op jit(solution)/shard_map/ppermute | solution.py:12
  62.9 49.0 %collective-permute-start.6 = (bf16[2048,512]{0,1:T(8,128)(2,1)}, bf16[2048,512]{0,1:T(8,128)(2,1)}, u32[]{:S(2)}, u32[]{:S(2)}) collective-permute-start(bf16[2048,512]{0,1:T(8,128)(2,1)} %copy.78), channel_id=1, source_target_pairs={{0,128},{64,192},{128,0},{192,64},{1,129},{65,193},{129,1},{193,65... | collective-permute-start | bytes 6291464 | tf_op jit(solution)/shard_map/ppermute | solution.py:12
  64.7 4.6 %copy-start = (f32[16,256,256]{2,1,0:T(8,128)S(1)}, f32[16,256,256]{2,1,0:T(8,128)}, u32[]{:S(2)}) copy-start(f32[16,256,256]{2,1,0:T(8,128)} %get-tuple-element.32) | copy-start | bytes 12582916
  69.3 10.8 %collective-permute-start.5 = (bf16[1,256,2048]{2,1,0:T(8,128)(2,1)}, bf16[1,256,2048]{2,1,0:T(8,128)(2,1)}, u32[]{:S(2)}, u32[]{:S(2)}) collective-permute-start(bf16[1,256,2048]{2,1,0:T(8,128)(2,1)} %collective-permute-done.3), channel_id=1, source_target_pairs={{0,64},{64,0},{128,192},{192,128},{1,65},{65,1},{129,193},{193,129... | collective-permute-start | bytes 3145736 | tf_op jit(solution)/shard_map/ppermute | solution.py:17
  69.3 6.3 %copy-start.1 = (f32[16,256,256]{2,1,0:T(8,128)S(1)}, f32[16,256,256]{2,1,0:T(8,128)}, u32[]{:S(2)}) copy-start(f32[16,256,256]{2,1,0:T(8,128)} %get-tuple-element.28) | copy-start | bytes 12582916
  69.3 6.3 %copy-start.4 = (bf16[1,256,2048]{1,2,0:T(8,128)(2,1)S(1)}, bf16[1,256,2048]{1,2,0:T(8,128)(2,1)}, u32[]{:S(2)}) copy-start(bf16[1,256,2048]{1,2,0:T(8,128)(2,1)} %copy.69) | copy-start | bytes 3145732
  75.6 2.3 copy-start.3
  88.0 3.0 %copy-start.6 = (bf16[1,256,2048]{2,1,0:T(8,128)(2,1)S(1)}, bf16[1,256,2048]{2,1,0:T(8,128)(2,1)}, u32[]{:S(2)}) copy-start(bf16[1,256,2048]{2,1,0:T(8,128)(2,1)} %param.12) | copy-start | bytes 3145732
  91.1 3.0 %copy-start.8 = (f32[2048]{0:T(1024)S(1)}, f32[2048]{0:T(1024)}, u32[]{:S(2)}) copy-start(f32[2048]{0:T(1024)} %param.13) | copy-start | bytes 24580
  93.1 1.0 copy-start.2
  111.9 74.2 %all-to-all-start = ((bf16[64,80,256]{2,1,0:T(8,128)(2,1)}), bf16[64,80,256]{2,1,0:T(8,128)(2,1)}, u32[]{:S(2)}, u32[]{:S(2)}) async-start(bf16[64,80,256]{2,1,0:T(8,128)(2,1)} %reshape.343), calls=%async_computation | async-start | bytes 5242880 | tf_op jit(solution)/shard_map/all_to_all | solution.py:99
  127.4 45.8 %collective-permute-start.7 = (bf16[2048,512]{0,1:T(8,128)(2,1)}, bf16[2048,512]{0,1:T(8,128)(2,1)S(1)}, u32[]{:S(2)}, u32[]{:S(2)}) collective-permute-start(bf16[2048,512]{0,1:T(8,128)(2,1)} %copy.80), channel_id=1, source_target_pairs={{0,64},{64,0},{128,192},{192,128},{1,65},{65,1},{129,193},{193,129... | collective-permute-start | bytes 6291464 | tf_op jit(solution)/shard_map/ppermute | solution.py:17
  127.4 45.8 %collective-permute-start.8 = (bf16[2048,512]{0,1:T(8,128)(2,1)}, bf16[2048,512]{0,1:T(8,128)(2,1)S(1)}, u32[]{:S(2)}, u32[]{:S(2)}) collective-permute-start(bf16[2048,512]{0,1:T(8,128)(2,1)} %collective-permute-done.6), channel_id=1, source_target_pairs={{0,64},{64,0},{128,192},{192,128},{1,65},{65,1},{129,193},{193,129... | collective-permute-start | bytes 6291464 | tf_op jit(solution)/shard_map/ppermute | solution.py:17
  127.9 45.2 %collective-permute-start.9 = (bf16[256,2048]{1,0:T(8,128)(2,1)}, bf16[256,2048]{1,0:T(8,128)(2,1)}, u32[]{:S(2)}, u32[]{:S(2)}) collective-permute-start(bf16[256,2048]{1,0:T(8,128)(2,1)} %bitcast.40), channel_id=1, source_target_pairs={{0,128},{64,192},{128,0},{192,64},{1,129},{65,193},{129,1},{193,65... | collective-permute-start | bytes 3145736 | tf_op jit(solution)/shard_map/ppermute | solution.py:12
  128.7 74.4 %collective-permute-start.10 = (bf16[256,2048]{1,0:T(8,128)(2,1)}, bf16[256,2048]{1,0:T(8,128)(2,1)}, u32[]{:S(2)}, u32[]{:S(2)}) collective-permute-start(bf16[256,2048]{1,0:T(8,128)(2,1)} %bitcast.40), channel_id=1, source_target_pairs={{0,64},{64,0},{128,192},{192,128},{1,65},{65,1},{129,193},{193,129... | collective-permute-start | bytes 3145736 | tf_op jit(solution)/shard_map/ppermute | solution.py:17
  173.1 32.1 %collective-permute-start.11 = (bf16[256,2048]{1,0:T(8,128)(2,1)}, bf16[256,2048]{1,0:T(8,128)(2,1)}, u32[]{:S(2)}, u32[]{:S(2)}) collective-permute-start(bf16[256,2048]{1,0:T(8,128)(2,1)} %collective-permute-done.9), channel_id=1, source_target_pairs={{0,64},{64,0},{128,192},{192,128},{1,65},{65,1},{129,193},{193,129... | collective-permute-start | bytes 3145736 | tf_op jit(solution)/shard_map/ppermute | solution.py:17
  210.9 6.9 %copy-start.9 = (f32[1,256,2]{1,2,0:T(2,128)S(1)}, f32[1,256,2]{1,2,0:T(2,128)}, u32[]{:S(2)}) copy-start(f32[1,256,2]{1,2,0:T(2,128)} %param.15) | copy-start | bytes 6148
  210.9 67.8 %all-to-all-start.1 = ((bf16[64,80,256]{2,1,0:T(8,128)(2,1)}), bf16[64,80,256]{2,1,0:T(8,128)(2,1)}, u32[]{:S(2)}, u32[]{:S(2)}) async-start(bf16[64,80,256]{2,1,0:T(8,128)(2,1)} %reshape.345), calls=%async_computation.1 | async-start | bytes 5242880 | tf_op jit(solution)/shard_map/all_to_all | solution.py:112

commit v4 on v2

--- a/solution.py
+++ b/solution.py
@@ -37,9 +37,9 @@
     local_units = down_weight.shape[1]
     gate_up_local = gate_up_weight[0].reshape(feature_count, 2 * local_units)
     down_local = down_weight[0]
-    key_far = far_block(key_rows)
-    value_far = far_block(value_rows, key_far)
-    gate_up_far = far_block(gate_up_local, value_far)
+    value_far = far_block(value_rows)
+    key_far = far_block(key_rows, value_far)
+    gate_up_far = far_block(gate_up_local, key_far)
     down_far = far_block(down_local, gate_up_far)
     key_blocks = near_blocks(key_rows, key_far)
     value_blocks = near_blocks(value_rows, value_far)

time: 291 us -> 298 us (1.024)
  waiting for transfers between devices: 157 us -> 176 us
  matrix products: 49.8 us -> 37.4 us
  local copies, waits for them, and re-layouts: 46.5 us -> 50.5 us
  other arithmetic: 12 us -> 8.6 us
    ppermute x4, waiting for transfers between devices: 80.1 us -> 97.9 us  [far_block(): return lax.ppermute(block, 'ctx', perm=[(c, c ^ 2) for c in range(4)])]
    dot_general x4, matrix products: 13.9 us -> 5.33 us  [shards(): jnp.einsum('cqhk,ckhd->cqhd', expo.astype(jnp.bfloat16), block.reshape(cl...]
    dot_general x4, matrix products: 14.7 us -> 10.9 us  [shards(): jnp.einsum('cqhd,ckhd->cqhk', query_heads, block.reshape(clip_count, -1,...]
    reduce_sum x1, other arithmetic: 6.23 us -> 2.85 us  [shards(): block_sum = jnp.sum(expo, axis=-1)]
    unnamed x31 -> x33, local copies, waits for them, and re-layouts: 10.4 us -> 13.1 us
  transfers between devices with their start and end apart: 14 -> 14, of which waited for: 6 -> 6; matrix products, arithmetic and copies ran while one was open for 30% -> 25% of each run, Pallas kernels for 0% -> 0%
where the time goes in v4:
time: 298 us; the launch traced here: 297 us
  waiting for transfers between devices  176 us (59%)
  local copies, waits for them, and re-layouts  50.5 us (17%)
  matrix products  37.4 us (13%)
  starting transfers between devices  24.1 us (8%)
  other arithmetic  8.6 us (3%)
    ppermute x4, waiting for transfers between devices, far_block(): return lax.ppermute(block, 'ctx', perm=[(c, c ^ 2) for c in range(4)])  97.9 us
    all_to_all x1, waiting for transfers between devices, shards(): lax.all_to_all(summed, 'exp', split_axis=0, concat_axis=0, tiled=True)  61.1 us
    all_to_all x1, waiting for transfers between devices, shards(): lax.all_to_all(send_buffer, 'exp', split_axis=0, concat_axis=0, tiled=True)  17 us
    dot_general x4, matrix products, shards(): jnp.dot(flattened, gate_up_block, preferred_element_type=jnp.float32)  13.4 us
    unnamed x33, local copies, waits for them, and re-layouts  13.1 us
    all_to_all x1, starting transfers between devices, shards(): lax.all_to_all(send_buffer, 'exp', split_axis=0, concat_axis=0, tiled=True)  12.7 us
    dot_general x4, matrix products, shards(): jnp.einsum('cqhd,ckhd->cqhk', query_heads, block.reshape(clip_count, -1,...  10.9 us
    dot_general x4, matrix products, shards(): group_part = jnp.dot(hidden, down_block, preferred_element_type=jnp.float32)  7.75 us
  transfers between devices with their start and end apart: 14, of which 6 were waited for; matrix products, arithmetic and copies ran while one was open for 25% of the time, Pallas kernels for 0%

profile of v4, /device:TPU:4, one launch (start us, length us, event | category | flops | bytes accessed | tf_op | source)
XLA Modules:
  0.0 297.1 jit_solution(5781219694419458084)
XLA Ops:
  7.2 19.4 %collective-permute-done = bf16[1,256,2048]{2,1,0:T(8,128)(2,1)S(1)} collective-permute-done((bf16[1,256,2048]{2,1,0:T(8,128)(2,1)}, bf16[1,256,2048]{2,1,0:T(8,128)(2,1)S(1)}, u32[]{:S(2)}, u32[]{:S(2)}) %collective-permute-start) | collective-permute-done | bytes 1048608 | tf_op jit(solution)/shard_map/ppermute | solution.py:12
  32.1 3.5 %copy.81 = bf16[256,8,2,256]{3,1,2,0:T(8,128)(2,1)} copy(bf16[256,8,2,256]{3,2,1,0:T(2,128)(2,1)} %bitcast.157) | data formatting | bytes 4194304
  38.3 15.5 %collective-permute-done.1 = bf16[1,256,2048]{1,2,0:T(8,128)(2,1)} collective-permute-done((bf16[1,256,2048]{1,2,0:T(8,128)(2,1)}, bf16[1,256,2048]{1,2,0:T(8,128)(2,1)}, u32[]{:S(2)}, u32[]{:S(2)}) %collective-permute-start.1) | collective-permute-done | bytes 1048608 | tf_op jit(solution)/shard_map/ppermute | solution.py:12
  53.8 2.7 bitcast_reduce_fusion.3
  60.3 4.0 %bitcast_reduce_fusion.1 = (f32[256,16]{0,1:T(8,128)S(1)}, f32[16,256,256]{2,1,0:T(8,128)}) fusion(bf16[256,16,128]{0,2,1:T(8,128)(2,1)} %bitcast.6, bf16[256,16,128]{2,1,0:T(8,128)(2,1)S(1)} %bitcast.147), kind=kOutput, calls=%fused_computation.9 | convolution fusion | flops 270528512 | bytes 6307840 | tf_op jit(solution)/shard_map/cqhd,ckhd->cqhk/dot_general | solution.py:47
  75.4 2.9 fusion.6
  79.5 2.6 bitcast_divide_fusion
  85.9 4.1 %gather_fusion = bf16[640,2048]{1,0:T(8,128)(2,1)} fusion(bf16[256,2048]{1,0:T(8,128)(2,1)S(1)} %fusion.37, s32[1024]{0:T(1024)S(1)} %pad_clamp_fusion.2), kind=kCustom, calls=%fused_computation | custom fusion | bytes 5245440 | tf_op jit(solution)/shard_map/gather | solution.py:94
  90.0 5.3 %reshape.337 = bf16[64,80,256]{2,1,0:T(8,128)(2,1)} reshape(bf16[640,2048]{1,0:T(8,128)(2,1)} %gather_fusion) | data formatting | bytes 5242880 | tf_op jit(solution)/shard_map/reshape | solution.py:95
  95.2 18.9 %collective-permute-done.6 = bf16[2048,512]{1,0:T(8,128)(2,1)} collective-permute-done((bf16[2048,512]{1,0:T(8,128)(2,1)}, bf16[2048,512]{1,0:T(8,128)(2,1)}, u32[]{:S(2)}, u32[]{:S(2)}) %collective-permute-start.6) | collective-permute-done | bytes 2097184 | tf_op jit(solution)/shard_map/ppermute | solution.py:12
  114.1 12.7 %all-to-all-start = ((bf16[64,80,256]{2,1,0:T(8,128)(2,1)}), bf16[64,80,256]{2,1,0:T(8,128)(2,1)S(1)}, u32[]{:S(2)}, u32[]{:S(2)}) async-start(bf16[64,80,256]{2,1,0:T(8,128)(2,1)} %reshape.337), calls=%async_computation | async-start | bytes 5242880 | tf_op jit(solution)/shard_map/all_to_all | solution.py:99
  128.3 44.1 %collective-permute-done.7 = bf16[256,2048]{1,0:T(8,128)(2,1)} collective-permute-done((bf16[256,2048]{1,0:T(8,128)(2,1)}, bf16[256,2048]{1,0:T(8,128)(2,1)}, u32[]{:S(2)}, u32[]{:S(2)}) %collective-permute-start.7) | collective-permute-done | bytes 1048608 | tf_op jit(solution)/shard_map/ppermute | solution.py:12
  172.4 17.0 %all-to-all-done = bf16[64,80,256]{2,1,0:T(8,128)(2,1)S(1)} async-done(((bf16[64,80,256]{2,1,0:T(8,128)(2,1)}), bf16[64,80,256]{2,1,0:T(8,128)(2,1)S(1)}, u32[]{:S(2)}, u32[]{:S(2)}) %all-to-all-start) | async-done | bytes 2621472 | tf_op jit(solution)/shard_map/all_to_all | solution.py:99
  189.4 3.1 %reshape.338 = bf16[640,2048]{1,0:T(8,128)(2,1)} reshape(bf16[64,80,256]{2,1,0:T(8,128)(2,1)S(1)} %all-to-all-done) | data formatting | bytes 5242880 | tf_op jit(solution)/shard_map/reshape | solution.py:100
  192.6 4.0 %fusion.82 = f32[640,512]{1,0:T(8,128)S(1)} fusion(bf16[640,2048]{1,0:T(8,128)(2,1)} %reshape.338, bf16[2048,512]{1,0:T(8,128)(2,1)} %collective-permute-done.6), kind=kOutput, calls=%fused_computation.122 | convolution fusion | flops 1342177280 | bytes 6029312 | tf_op jit(solution)/shard_map/dot_general | solution.py:103
  196.6 3.2 %fusion.81 = f32[640,512]{1,0:T(8,128)S(1)} fusion(bf16[640,2048]{1,0:T(8,128)(2,1)S(1)} %copy-done.7, bf16[2048,512]{1,0:T(8,128)(2,1)} %bitcast.52), kind=kOutput, calls=%fused_computation.121 | convolution fusion | flops 1342177280 | bytes 6029312 | tf_op jit(solution)/shard_map/dot_general | solution.py:103
  200.7 3.1 %fusion.83 = f32[640,512]{1,0:T(8,128)S(1)} fusion(bf16[640,2048]{1,0:T(8,128)(2,1)S(1)} %copy-done.7, bf16[2048,512]{1,0:T(8,128)(2,1)} %collective-permute-done.8), kind=kOutput, calls=%fused_computation.123 | convolution fusion | flops 1342177280 | bytes 6029312 | tf_op jit(solution)/shard_map/dot_general | solution.py:103
  208.1 3.1 %fusion.84 = f32[640,512]{1,0:T(8,128)S(1)} fusion(bf16[640,2048]{1,0:T(8,128)(2,1)S(1)} %copy-done.7, bf16[2048,512]{1,0:T(8,128)(2,1)} %collective-permute-done.10), kind=kOutput, calls=%fused_computation.124 | convolution fusion | flops 1342177280 | bytes 6029312 | tf_op jit(solution)/shard_map/dot_general | solution.py:103
  211.2 2.7 add_convert_fusion
  213.9 3.2 %reshape.339 = bf16[64,80,256]{2,1,0:T(8,128)(2,1)} reshape(bf16[640,2048]{1,0:T(8,128)(2,1)S(1)} %add_convert_fusion) | data formatting | bytes 5242880 | tf_op jit(solution)/shard_map/reshape | solution.py:110
  217.1 6.5 %all-to-all-start.1 = ((bf16[64,80,256]{2,1,0:T(8,128)(2,1)}), bf16[64,80,256]{2,1,0:T(8,128)(2,1)}, u32[]{:S(2)}, u32[]{:S(2)}) async-start(bf16[64,80,256]{2,1,0:T(8,128)(2,1)} %reshape.339), calls=%async_computation.1 | async-start | bytes 5242880 | tf_op jit(solution)/shard_map/all_to_all | solution.py:111
  224.0 61.1 %all-to-all-done.1 = bf16[64,80,256]{2,1,0:T(8,128)(2,1)} async-done(((bf16[64,80,256]{2,1,0:T(8,128)(2,1)}), bf16[64,80,256]{2,1,0:T(8,128)(2,1)}, u32[]{:S(2)}, u32[]{:S(2)}) %all-to-all-start.1) | async-done | bytes 2621472 | tf_op jit(solution)/shard_map/all_to_all | solution.py:111
  285.0 3.9 %reshape.340 = bf16[640,2048]{1,0:T(8,128)(2,1)S(1)} reshape(bf16[64,80,256]{2,1,0:T(8,128)(2,1)} %all-to-all-done.1) | data formatting | bytes 5242880 | tf_op jit(solution)/shard_map/reshape | solution.py:112
  293.7 3.4 %fusion.15 = bf16[1,256,2048]{2,1,0:T(8,128)(2,1)} fusion(bf16[1,256,2048]{2,1,0:T(8,128)(2,1)} %copy-done.3, bf16[256,2048]{1,0:T(8,128)(2,1)} %gather_fusion.2, bf16[256,2048]{1,0:T(8,128)(2,1)} %gather_fusion.1, f32[256]{0:T(256)S(1)} %bitcast.161, f32[256]{0:T(256)S(1)} %bitcast.160), kind=kLoop, calls=%fused_computation.35 | loop fusion | flops 4194304 | bytes 4196352 | tf_op jit(solution)/shard_map/convert_element_type | solution.py:119
  (94 shorter events, 46.6 us)
Async XLA Ops:
  0.0 28.5 %copy-start.9 = (bf16[1,256,2048]{2,1,0:T(8,128)(2,1)S(1)}, bf16[1,256,2048]{2,1,0:T(8,128)(2,1)}, u32[]{:S(2)}) copy-start(bf16[1,256,2048]{2,1,0:T(8,128)(2,1)} %param.11) | copy-start | bytes 3145732
  0.0 26.6 %copy-start.2 = (bf16[1,256,2048]{2,1,0:T(8,128)(2,1)S(1)}, bf16[1,256,2048]{2,1,0:T(8,128)(2,1)}, u32[]{:S(2)}) copy-start(bf16[1,256,2048]{2,1,0:T(8,128)(2,1)} %param.10) | copy-start | bytes 3145732
  0.0 26.6 %collective-permute-start = (bf16[1,256,2048]{2,1,0:T(8,128)(2,1)}, bf16[1,256,2048]{2,1,0:T(8,128)(2,1)S(1)}, u32[]{:S(2)}, u32[]{:S(2)}) collective-permute-start(bf16[1,256,2048]{2,1,0:T(8,128)(2,1)} %param.11), channel_id=1, source_target_pairs={{0,128},{64,192},{128,0},{192,64},{1,129},{65,193},{129,1},{193,65... | collective-permute-start | bytes 3145736 | tf_op jit(solution)/shard_map/ppermute | solution.py:12
  2.2 56.6 %collective-permute-start.4 = (bf16[1,256,2048]{2,1,0:T(8,128)(2,1)}, bf16[1,256,2048]{2,1,0:T(8,128)(2,1)}, u32[]{:S(2)}, u32[]{:S(2)}) collective-permute-start(bf16[1,256,2048]{2,1,0:T(8,128)(2,1)} %param.11), channel_id=1, source_target_pairs={{0,64},{64,0},{128,192},{192,128},{1,65},{65,1},{129,193},{193,129... | collective-permute-start | bytes 3145736 | tf_op jit(solution)/shard_map/ppermute | solution.py:17
  4.5 55.8 %collective-permute-start.2 = (bf16[1,256,2048]{1,2,0:T(8,128)(2,1)}, bf16[1,256,2048]{1,2,0:T(8,128)(2,1)}, u32[]{:S(2)}, u32[]{:S(2)}) collective-permute-start(bf16[1,256,2048]{1,2,0:T(8,128)(2,1)} %copy.52), channel_id=1, source_target_pairs={{0,64},{64,0},{128,192},{192,128},{1,65},{65,1},{129,193},{193,129... | collective-permute-start | bytes 3145736 | tf_op jit(solution)/shard_map/ppermute | solution.py:17
  27.9 25.9 %collective-permute-start.1 = (bf16[1,256,2048]{1,2,0:T(8,128)(2,1)}, bf16[1,256,2048]{1,2,0:T(8,128)(2,1)}, u32[]{:S(2)}, u32[]{:S(2)}) collective-permute-start(bf16[1,256,2048]{1,2,0:T(8,128)(2,1)} %copy.49), channel_id=1, source_target_pairs={{0,128},{64,192},{128,0},{192,64},{1,129},{65,193},{129,1},{193,65... | collective-permute-start | bytes 3145736 | tf_op jit(solution)/shard_map/ppermute | solution.py:12
  31.9 21.9 %copy-start.5 = (bf16[32,8,16,128]{3,2,1,0:T(8,128)(2,1)S(1)}, bf16[32,8,16,128]{3,2,1,0:T(8,128)(2,1)}, u32[]{:S(2)}) copy-start(bf16[32,8,16,128]{3,2,1,0:T(8,128)(2,1)} %copy.79) | copy-start | bytes 3145732
  38.2 26.4 %collective-permute-start.5 = (bf16[1,256,2048]{2,1,0:T(8,128)(2,1)}, bf16[1,256,2048]{2,1,0:T(8,128)(2,1)}, u32[]{:S(2)}, u32[]{:S(2)}) collective-permute-start(bf16[1,256,2048]{2,1,0:T(8,128)(2,1)} %copy-done.10), channel_id=1, source_target_pairs={{0,64},{64,0},{128,192},{192,128},{1,65},{65,1},{129,193},{193,129... | collective-permute-start | bytes 3145736 | tf_op jit(solution)/shard_map/ppermute | solution.py:17
  53.8 15.1 %collective-permute-start.3 = (bf16[1,256,2048]{1,2,0:T(8,128)(2,1)}, bf16[1,256,2048]{1,2,0:T(8,128)(2,1)}, u32[]{:S(2)}, u32[]{:S(2)}) collective-permute-start(bf16[1,256,2048]{1,2,0:T(8,128)(2,1)} %collective-permute-done.1), channel_id=1, source_target_pairs={{0,64},{64,0},{128,192},{192,128},{1,65},{65,1},{129,193},{193,129... | collective-permute-start | bytes 3145736 | tf_op jit(solution)/shard_map/ppermute | solution.py:17
  64.3 49.9 %collective-permute-start.6 = (bf16[2048,512]{1,0:T(8,128)(2,1)}, bf16[2048,512]{1,0:T(8,128)(2,1)}, u32[]{:S(2)}, u32[]{:S(2)}) collective-permute-start(bf16[2048,512]{1,0:T(8,128)(2,1)} %bitcast.52), channel_id=1, source_target_pairs={{0,128},{64,192},{128,0},{192,64},{1,129},{65,193},{129,1},{193,65... | collective-permute-start | bytes 6291464 | tf_op jit(solution)/shard_map/ppermute | solution.py:12
  68.9 2.2 copy-start.4
  71.1 2.2 copy-start
  73.3 2.2 copy-start.1
  82.1 2.0 copy-start.8
  114.1 75.3 %all-to-all-start = ((bf16[64,80,256]{2,1,0:T(8,128)(2,1)}), bf16[64,80,256]{2,1,0:T(8,128)(2,1)S(1)}, u32[]{:S(2)}, u32[]{:S(2)}) async-start(bf16[64,80,256]{2,1,0:T(8,128)(2,1)} %reshape.337), calls=%async_computation | async-start | bytes 5242880 | tf_op jit(solution)/shard_map/all_to_all | solution.py:99
  126.9 45.5 %collective-permute-start.7 = (bf16[256,2048]{1,0:T(8,128)(2,1)}, bf16[256,2048]{1,0:T(8,128)(2,1)}, u32[]{:S(2)}, u32[]{:S(2)}) collective-permute-start(bf16[256,2048]{1,0:T(8,128)(2,1)} %bitcast.164), channel_id=1, source_target_pairs={{0,128},{64,192},{128,0},{192,64},{1,129},{65,193},{129,1},{193,65... | collective-permute-start | bytes 3145736 | tf_op jit(solution)/shard_map/ppermute | solution.py:12
  127.8 72.9 %collective-permute-start.8 = (bf16[2048,512]{1,0:T(8,128)(2,1)}, bf16[2048,512]{1,0:T(8,128)(2,1)}, u32[]{:S(2)}, u32[]{:S(2)}) collective-permute-start(bf16[2048,512]{1,0:T(8,128)(2,1)} %bitcast.52), channel_id=1, source_target_pairs={{0,64},{64,0},{128,192},{192,128},{1,65},{65,1},{129,193},{193,129... | collective-permute-start | bytes 6291464 | tf_op jit(solution)/shard_map/ppermute | solution.py:17
  127.8 78.2 %collective-permute-start.9 = (bf16[256,2048]{1,0:T(8,128)(2,1)}, bf16[256,2048]{1,0:T(8,128)(2,1)}, u32[]{:S(2)}, u32[]{:S(2)}) collective-permute-start(bf16[256,2048]{1,0:T(8,128)(2,1)} %bitcast.165), channel_id=1, source_target_pairs={{0,64},{64,0},{128,192},{192,128},{1,65},{65,1},{129,193},{193,129... | collective-permute-start | bytes 3145736 | tf_op jit(solution)/shard_map/ppermute | solution.py:17
  128.3 79.8 %collective-permute-start.10 = (bf16[2048,512]{1,0:T(8,128)(2,1)}, bf16[2048,512]{1,0:T(8,128)(2,1)}, u32[]{:S(2)}, u32[]{:S(2)}) collective-permute-start(bf16[2048,512]{1,0:T(8,128)(2,1)} %collective-permute-done.6), channel_id=1, source_target_pairs={{0,64},{64,0},{128,192},{192,128},{1,65},{65,1},{129,193},{193,129... | collective-permute-start | bytes 6291464 | tf_op jit(solution)/shard_map/ppermute | solution.py:17
  172.4 38.8 %collective-permute-start.11 = (bf16[256,2048]{1,0:T(8,128)(2,1)}, bf16[256,2048]{1,0:T(8,128)(2,1)}, u32[]{:S(2)}, u32[]{:S(2)}) collective-permute-start(bf16[256,2048]{1,0:T(8,128)(2,1)} %collective-permute-done.7), channel_id=1, source_target_pairs={{0,64},{64,0},{128,192},{192,128},{1,65},{65,1},{129,193},{193,129... | collective-permute-start | bytes 3145736 | tf_op jit(solution)/shard_map/ppermute | solution.py:17
  192.6 4.0 %copy-start.7 = (bf16[640,2048]{1,0:T(8,128)(2,1)S(1)}, bf16[640,2048]{1,0:T(8,128)(2,1)}, u32[]{:S(2)}) copy-start(bf16[640,2048]{1,0:T(8,128)(2,1)} %reshape.338) | copy-start | bytes 7864324
  196.6 3.2 %copy-start.13 = (bf16[1,256,2048]{2,1,0:T(8,128)(2,1)S(1)}, bf16[1,256,2048]{2,1,0:T(8,128)(2,1)}, u32[]{:S(2)}) copy-start(bf16[1,256,2048]{2,1,0:T(8,128)(2,1)} %param.17) | copy-start | bytes 3145732
  217.1 6.9 %copy-start.12 = (f32[1,256,2]{1,2,0:T(2,128)S(1)}, f32[1,256,2]{1,2,0:T(2,128)}, u32[]{:S(2)}) copy-start(f32[1,256,2]{1,2,0:T(2,128)} %param.15) | copy-start | bytes 6148
  217.1 68.0 %all-to-all-start.1 = ((bf16[64,80,256]{2,1,0:T(8,128)(2,1)}), bf16[64,80,256]{2,1,0:T(8,128)(2,1)}, u32[]{:S(2)}, u32[]{:S(2)}) async-start(bf16[64,80,256]{2,1,0:T(8,128)(2,1)} %reshape.339), calls=%async_computation.1 | async-start | bytes 5242880 | tf_op jit(solution)/shard_map/all_to_all | solution.py:111
  (4 other events, 5.3 us)

commit v5 on v2

--- a/solution.py
+++ b/solution.py
@@ -38,7 +38,7 @@
     gate_up_local = gate_up_weight[0].reshape(feature_count, 2 * local_units)
     down_local = down_weight[0]
     key_far = far_block(key_rows)
-    value_far = far_block(value_rows, key_far)
+    value_far = far_block(value_rows)
     gate_up_far = far_block(gate_up_local, value_far)
     down_far = far_block(down_local, gate_up_far)
     key_blocks = near_blocks(key_rows, key_far)

time: 291 us -> 282 us (0.969)
  matrix products: 49.8 us -> 41.4 us
    dot_general x4, matrix products: 14.7 us -> 8.98 us  [shards(): jnp.einsum('cqhd,ckhd->cqhk', query_heads, block.reshape(clip_count, -1,...]
    reduce_sum x1, other arithmetic: 6.23 us -> 2.84 us  [shards(): block_sum = jnp.sum(expo, axis=-1)]
    unnamed x31 -> x29, local copies, waits for them, and re-layouts: 10.4 us -> 9.97 us
  transfers between devices with their start and end apart: 14 -> 14, of which waited for: 6 -> 6; matrix products, arithmetic and copies ran while one was open for 30% -> 28% of each run, Pallas kernels for 0% -> 0%
where the time goes in v5:
time: 282 us; the launch traced here: 281 us
  waiting for transfers between devices  157 us (56%)
  local copies, waits for them, and re-layouts  46.1 us (16%)
  matrix products  41.4 us (15%)
  starting transfers between devices  25 us (9%)
  other arithmetic  10.7 us (4%)
    ppermute x4, waiting for transfers between devices, far_block(): return lax.ppermute(block, 'ctx', perm=[(c, c ^ 2) for c in range(4)])  81.7 us
    all_to_all x1, waiting for transfers between devices, shards(): lax.all_to_all(summed, 'exp', split_axis=0, concat_axis=0, tiled=True)  60.4 us
    all_to_all x1, waiting for transfers between devices, shards(): lax.all_to_all(send_buffer, 'exp', split_axis=0, concat_axis=0, tiled=True)  15 us
    dot_general x4, matrix products, shards(): jnp.dot(flattened, gate_up_block, preferred_element_type=jnp.float32)  13.4 us
    all_to_all x1, starting transfers between devices, shards(): lax.all_to_all(send_buffer, 'exp', split_axis=0, concat_axis=0, tiled=True)  12.7 us
    dot_general x4, matrix products, shards(): jnp.einsum('cqhk,ckhd->cqhd', expo.astype(jnp.bfloat16), block.reshape(cl...  11.2 us
    unnamed x29, local copies, waits for them, and re-layouts  9.97 us
    dot_general x4, matrix products, shards(): jnp.einsum('cqhd,ckhd->cqhk', query_heads, block.reshape(clip_count, -1,...  8.98 us
  transfers between devices with their start and end apart: 14, of which 6 were waited for; matrix products, arithmetic and copies ran while one was open for 28% of the time, Pallas kernels for 0%

profile of v5, /device:TPU:4, one launch (start us, length us, event | category | flops | bytes accessed | tf_op | source)
XLA Modules:
  0.0 280.7 jit_solution(8279027093729258976)
XLA Ops:
  12.1 3.5 %copy.81 = bf16[256,8,2,256]{3,1,2,0:T(8,128)(2,1)} copy(bf16[256,8,2,256]{3,2,1,0:T(2,128)(2,1)} %bitcast.157) | data formatting | bytes 4194304
  15.8 2.4 scatter_custom_fusion
  18.3 12.0 %collective-permute-done = bf16[1,256,2048]{1,2,0:T(8,128)(2,1)} collective-permute-done((bf16[1,256,2048]{1,2,0:T(8,128)(2,1)}, bf16[1,256,2048]{1,2,0:T(8,128)(2,1)}, u32[]{:S(2)}, u32[]{:S(2)}) %collective-permute-start) | collective-permute-done | bytes 1048608 | tf_op jit(solution)/shard_map/ppermute | solution.py:12
  30.2 2.7 bitcast_reduce_fusion.3
  32.9 18.6 %collective-permute-done.3 = bf16[1,256,2048]{2,1,0:T(8,128)(2,1)} collective-permute-done((bf16[1,256,2048]{2,1,0:T(8,128)(2,1)}, bf16[1,256,2048]{2,1,0:T(8,128)(2,1)}, u32[]{:S(2)}, u32[]{:S(2)}) %collective-permute-start.3) | collective-permute-done | bytes 1048608 | tf_op jit(solution)/shard_map/ppermute | solution.py:12
  63.0 2.8 %fusion.6 = (f32[256,16]{0,1:T(8,128)S(1)}, f32[256,16]{0,1:T(8,128)S(1)}, f32[256,16]{0,1:T(8,128)S(1)}, f32[256,16]{0,1:T(8,128)S(1)}) fusion(f32[16,256,256]{2,1,0:T(8,128)S(1)} %get-tuple-element.28, f32[256,16]{0,1:T(8,128)S(1)} %maximum_maximum_fusion, f32[16,256,256]{2,1,0:T(8,128)S(1)} %copy-done, f32[16,256,256]{2,1,0:T(8,128)S(1)} %get-tuple-element.26, ...), kind=kLoop, calls=%fused_computation.19 | loop fusion | flops 12566528 | bytes 16859136 | tf_op jit(solution)/shard_map/reduce_sum | solution.py:63
  73.1 5.8 %bitcast_divide_fusion = f32[1,256,16,128]{1,3,2,0:T(8,128)} fusion(f32[16,256,128]{1,2,0:T(8,128)} %fusion.20, f32[16,256,128]{1,2,0:T(8,128)} %fusion.26, f32[16,256,128]{1,2,0:T(8,128)S(1)} %fusion.23, f32[256,16]{0,1:T(8,128)S(1)} %add_add_fusion, bf16[256,16,128]{0,2,1:T(8,128)(2,1)S(1)} %bitcast.156, f32[16,256,256]{2,1,0:T(8,128)} %copy-done.1, ...), kind=kOutput, calls=%fused_computation.47 | convolution fusion | flops 273678336 | bytes 13664256 | tf_op jit(solution)/shard_map/cqhk,ckhd->cqhd/dot_general | solution.py:64
  83.8 4.1 %gather_fusion = bf16[640,2048]{1,0:T(8,128)(2,1)} fusion(bf16[256,2048]{1,0:T(8,128)(2,1)S(1)} %fusion.37, s32[1024]{0:T(1024)S(1)} %pad_clamp_fusion.2), kind=kCustom, calls=%fused_computation | custom fusion | bytes 5245440 | tf_op jit(solution)/shard_map/gather | solution.py:94
  87.9 5.3 %reshape.337 = bf16[64,80,256]{2,1,0:T(8,128)(2,1)} reshape(bf16[640,2048]{1,0:T(8,128)(2,1)} %gather_fusion) | data formatting | bytes 5242880 | tf_op jit(solution)/shard_map/reshape | solution.py:95
  93.1 6.7 %collective-permute-done.6 = bf16[2048,512]{1,0:T(8,128)(2,1)} collective-permute-done((bf16[2048,512]{1,0:T(8,128)(2,1)}, bf16[2048,512]{1,0:T(8,128)(2,1)}, u32[]{:S(2)}, u32[]{:S(2)}) %collective-permute-start.6) | collective-permute-done | bytes 2097184 | tf_op jit(solution)/shard_map/ppermute | solution.py:12
  99.9 12.7 %all-to-all-start = ((bf16[64,80,256]{2,1,0:T(8,128)(2,1)}), bf16[64,80,256]{2,1,0:T(8,128)(2,1)S(1)}, u32[]{:S(2)}, u32[]{:S(2)}) async-start(bf16[64,80,256]{2,1,0:T(8,128)(2,1)} %reshape.337), calls=%async_computation | async-start | bytes 5242880 | tf_op jit(solution)/shard_map/all_to_all | solution.py:99
  114.0 44.3 %collective-permute-done.7 = bf16[256,2048]{1,0:T(8,128)(2,1)} collective-permute-done((bf16[256,2048]{1,0:T(8,128)(2,1)}, bf16[256,2048]{1,0:T(8,128)(2,1)}, u32[]{:S(2)}, u32[]{:S(2)}) %collective-permute-start.7) | collective-permute-done | bytes 1048608 | tf_op jit(solution)/shard_map/ppermute | solution.py:12
  158.4 15.0 %all-to-all-done = bf16[64,80,256]{2,1,0:T(8,128)(2,1)S(1)} async-done(((bf16[64,80,256]{2,1,0:T(8,128)(2,1)}), bf16[64,80,256]{2,1,0:T(8,128)(2,1)S(1)}, u32[]{:S(2)}, u32[]{:S(2)}) %all-to-all-start) | async-done | bytes 2621472 | tf_op jit(solution)/shard_map/all_to_all | solution.py:99
  173.4 3.1 %reshape.338 = bf16[640,2048]{1,0:T(8,128)(2,1)} reshape(bf16[64,80,256]{2,1,0:T(8,128)(2,1)S(1)} %all-to-all-done) | data formatting | bytes 5242880 | tf_op jit(solution)/shard_map/reshape | solution.py:100
  176.5 4.0 %fusion.82 = f32[640,512]{1,0:T(8,128)S(1)} fusion(bf16[640,2048]{1,0:T(8,128)(2,1)} %reshape.338, bf16[2048,512]{1,0:T(8,128)(2,1)} %collective-permute-done.6), kind=kOutput, calls=%fused_computation.122 | convolution fusion | flops 1342177280 | bytes 6029312 | tf_op jit(solution)/shard_map/dot_general | solution.py:103
  180.6 3.2 %fusion.81 = f32[640,512]{1,0:T(8,128)S(1)} fusion(bf16[640,2048]{1,0:T(8,128)(2,1)S(1)} %copy-done.6, bf16[2048,512]{1,0:T(8,128)(2,1)} %bitcast.52), kind=kOutput, calls=%fused_computation.121 | convolution fusion | flops 1342177280 | bytes 6029312 | tf_op jit(solution)/shard_map/dot_general | solution.py:103
  184.7 3.1 %fusion.83 = f32[640,512]{1,0:T(8,128)S(1)} fusion(bf16[640,2048]{1,0:T(8,128)(2,1)S(1)} %copy-done.6, bf16[2048,512]{1,0:T(8,128)(2,1)} %collective-permute-done.8), kind=kOutput, calls=%fused_computation.123 | convolution fusion | flops 1342177280 | bytes 6029312 | tf_op jit(solution)/shard_map/dot_general | solution.py:103
  192.0 3.1 %fusion.84 = f32[640,512]{1,0:T(8,128)S(1)} fusion(bf16[640,2048]{1,0:T(8,128)(2,1)S(1)} %copy-done.6, bf16[2048,512]{1,0:T(8,128)(2,1)} %collective-permute-done.10), kind=kOutput, calls=%fused_computation.124 | convolution fusion | flops 1342177280 | bytes 6029312 | tf_op jit(solution)/shard_map/dot_general | solution.py:103
  195.2 2.7 add_convert_fusion
  197.8 3.2 %reshape.339 = bf16[64,80,256]{2,1,0:T(8,128)(2,1)} reshape(bf16[640,2048]{1,0:T(8,128)(2,1)S(1)} %add_convert_fusion) | data formatting | bytes 5242880 | tf_op jit(solution)/shard_map/reshape | solution.py:110
  201.0 6.8 %all-to-all-start.1 = ((bf16[64,80,256]{2,1,0:T(8,128)(2,1)}), bf16[64,80,256]{2,1,0:T(8,128)(2,1)}, u32[]{:S(2)}, u32[]{:S(2)}) async-start(bf16[64,80,256]{2,1,0:T(8,128)(2,1)} %reshape.339), calls=%async_computation.1 | async-start | bytes 5242880 | tf_op jit(solution)/shard_map/all_to_all | solution.py:111
  208.2 60.4 %all-to-all-done.1 = bf16[64,80,256]{2,1,0:T(8,128)(2,1)} async-done(((bf16[64,80,256]{2,1,0:T(8,128)(2,1)}), bf16[64,80,256]{2,1,0:T(8,128)(2,1)}, u32[]{:S(2)}, u32[]{:S(2)}) %all-to-all-start.1) | async-done | bytes 2621472 | tf_op jit(solution)/shard_map/all_to_all | solution.py:111
  268.7 3.9 %reshape.340 = bf16[640,2048]{1,0:T(8,128)(2,1)S(1)} reshape(bf16[64,80,256]{2,1,0:T(8,128)(2,1)} %all-to-all-done.1) | data formatting | bytes 5242880 | tf_op jit(solution)/shard_map/reshape | solution.py:112
  277.3 3.4 %fusion.15 = bf16[1,256,2048]{2,1,0:T(8,128)(2,1)} fusion(bf16[1,256,2048]{2,1,0:T(8,128)(2,1)} %get-tuple-element.20, bf16[256,2048]{1,0:T(8,128)(2,1)} %gather_fusion.2, bf16[256,2048]{1,0:T(8,128)(2,1)} %gather_fusion.1, f32[256]{0:T(256)S(1)} %bitcast.161, f32[256]{0:T(256)S(1)} %bitcast.160), kind=kLoop, calls=%fused_computation.35 | loop fusion | flops 4194304 | bytes 4196352 | tf_op jit(solution)/shard_map/convert_element_type | solution.py:119
  (89 shorter events, 47.2 us)
Async XLA Ops:
  0.0 8.6 %copy-start.8 = (bf16[1,256,2048]{2,1,0:T(8,128)(2,1)S(1)}, bf16[1,256,2048]{2,1,0:T(8,128)(2,1)}, u32[]{:S(2)}) copy-start(bf16[1,256,2048]{2,1,0:T(8,128)(2,1)} %param.11) | copy-start | bytes 3145732
  2.4 27.8 %collective-permute-start = (bf16[1,256,2048]{1,2,0:T(8,128)(2,1)}, bf16[1,256,2048]{1,2,0:T(8,128)(2,1)}, u32[]{:S(2)}, u32[]{:S(2)}) collective-permute-start(bf16[1,256,2048]{1,2,0:T(8,128)(2,1)} %copy.49), channel_id=1, source_target_pairs={{0,128},{64,192},{128,0},{192,64},{1,129},{65,193},{129,1},{193,65... | collective-permute-start | bytes 3145736 | tf_op jit(solution)/shard_map/ppermute | solution.py:12
  4.6 53.9 %collective-permute-start.1 = (bf16[1,256,2048]{1,2,0:T(8,128)(2,1)}, bf16[1,256,2048]{1,2,0:T(8,128)(2,1)}, u32[]{:S(2)}, u32[]{:S(2)}) collective-permute-start(bf16[1,256,2048]{1,2,0:T(8,128)(2,1)} %copy.49), channel_id=1, source_target_pairs={{0,64},{64,0},{128,192},{192,128},{1,65},{65,1},{129,193},{193,129... | collective-permute-start | bytes 3145736 | tf_op jit(solution)/shard_map/ppermute | solution.py:17
  4.6 47.0 %collective-permute-start.3 = (bf16[1,256,2048]{2,1,0:T(8,128)(2,1)}, bf16[1,256,2048]{2,1,0:T(8,128)(2,1)}, u32[]{:S(2)}, u32[]{:S(2)}) collective-permute-start(bf16[1,256,2048]{2,1,0:T(8,128)(2,1)} %param.11), channel_id=1, source_target_pairs={{0,128},{64,192},{128,0},{192,64},{1,129},{65,193},{129,1},{193,65... | collective-permute-start | bytes 3145736 | tf_op jit(solution)/shard_map/ppermute | solution.py:12
  5.9 48.2 %collective-permute-start.4 = (bf16[1,256,2048]{2,1,0:T(8,128)(2,1)}, bf16[1,256,2048]{2,1,0:T(8,128)(2,1)}, u32[]{:S(2)}, u32[]{:S(2)}) collective-permute-start(bf16[1,256,2048]{2,1,0:T(8,128)(2,1)} %param.11), channel_id=1, source_target_pairs={{0,64},{64,0},{128,192},{192,128},{1,65},{65,1},{129,193},{193,129... | collective-permute-start | bytes 3145736 | tf_op jit(solution)/shard_map/ppermute | solution.py:17
  6.9 3.8 %copy-start.4 = (bf16[1,256,2048]{2,1,0:T(8,128)(2,1)S(1)}, bf16[1,256,2048]{2,1,0:T(8,128)(2,1)}, u32[]{:S(2)}) copy-start(bf16[1,256,2048]{2,1,0:T(8,128)(2,1)} %param.10) | copy-start | bytes 3145732
  11.9 18.3 %copy-start.5 = (bf16[32,8,16,128]{3,2,1,0:T(8,128)(2,1)S(1)}, bf16[32,8,16,128]{3,2,1,0:T(8,128)(2,1)}, u32[]{:S(2)}) copy-start(bf16[32,8,16,128]{3,2,1,0:T(8,128)(2,1)} %copy.79) | copy-start | bytes 3145732
  30.2 30.3 %collective-permute-start.2 = (bf16[1,256,2048]{1,2,0:T(8,128)(2,1)}, bf16[1,256,2048]{1,2,0:T(8,128)(2,1)}, u32[]{:S(2)}, u32[]{:S(2)}) collective-permute-start(bf16[1,256,2048]{1,2,0:T(8,128)(2,1)} %collective-permute-done), channel_id=1, source_target_pairs={{0,64},{64,0},{128,192},{192,128},{1,65},{65,1},{129,193},{193,129... | collective-permute-start | bytes 3145736 | tf_op jit(solution)/shard_map/ppermute | solution.py:17
  51.6 48.3 %collective-permute-start.6 = (bf16[2048,512]{1,0:T(8,128)(2,1)}, bf16[2048,512]{1,0:T(8,128)(2,1)}, u32[]{:S(2)}, u32[]{:S(2)}) collective-permute-start(bf16[2048,512]{1,0:T(8,128)(2,1)} %bitcast.52), channel_id=1, source_target_pairs={{0,128},{64,192},{128,0},{192,64},{1,129},{65,193},{129,1},{193,65... | collective-permute-start | bytes 6291464 | tf_op jit(solution)/shard_map/ppermute | solution.py:12
  54.1 17.5 %collective-permute-start.5 = (bf16[1,256,2048]{2,1,0:T(8,128)(2,1)}, bf16[1,256,2048]{2,1,0:T(8,128)(2,1)}, u32[]{:S(2)}, u32[]{:S(2)}) collective-permute-start(bf16[1,256,2048]{2,1,0:T(8,128)(2,1)} %collective-permute-done.3), channel_id=1, source_target_pairs={{0,64},{64,0},{128,192},{192,128},{1,65},{65,1},{129,193},{193,129... | collective-permute-start | bytes 3145736 | tf_op jit(solution)/shard_map/ppermute | solution.py:17
  60.5 2.5 copy-start
  62.7 3.1 %copy-start.1 = (f32[16,256,256]{2,1,0:T(8,128)}, f32[16,256,256]{2,1,0:T(8,128)S(1)}, u32[]{:S(2)}) copy-start(f32[16,256,256]{2,1,0:T(8,128)S(1)} %get-tuple-element.24) | copy-start | bytes 12582916
  63.0 2.9 %copy-start.2 = (bf16[1,256,2048]{1,2,0:T(8,128)(2,1)S(1)}, bf16[1,256,2048]{1,2,0:T(8,128)(2,1)}, u32[]{:S(2)}) copy-start(bf16[1,256,2048]{1,2,0:T(8,128)(2,1)} %copy.59) | copy-start | bytes 3145732
  78.9 2.0 copy-start.7
  99.9 73.5 %all-to-all-start = ((bf16[64,80,256]{2,1,0:T(8,128)(2,1)}), bf16[64,80,256]{2,1,0:T(8,128)(2,1)S(1)}, u32[]{:S(2)}, u32[]{:S(2)}) async-start(bf16[64,80,256]{2,1,0:T(8,128)(2,1)} %reshape.337), calls=%async_computation | async-start | bytes 5242880 | tf_op jit(solution)/shard_map/all_to_all | solution.py:99
  112.6 45.7 %collective-permute-start.7 = (bf16[256,2048]{1,0:T(8,128)(2,1)}, bf16[256,2048]{1,0:T(8,128)(2,1)}, u32[]{:S(2)}, u32[]{:S(2)}) collective-permute-start(bf16[256,2048]{1,0:T(8,128)(2,1)} %bitcast.164), channel_id=1, source_target_pairs={{0,128},{64,192},{128,0},{192,64},{1,129},{65,193},{129,1},{193,65... | collective-permute-start | bytes 3145736 | tf_op jit(solution)/shard_map/ppermute | solution.py:12
  113.5 71.2 %collective-permute-start.8 = (bf16[2048,512]{1,0:T(8,128)(2,1)}, bf16[2048,512]{1,0:T(8,128)(2,1)}, u32[]{:S(2)}, u32[]{:S(2)}) collective-permute-start(bf16[2048,512]{1,0:T(8,128)(2,1)} %bitcast.52), channel_id=1, source_target_pairs={{0,64},{64,0},{128,192},{192,128},{1,65},{65,1},{129,193},{193,129... | collective-permute-start | bytes 6291464 | tf_op jit(solution)/shard_map/ppermute | solution.py:17
  113.5 76.4 %collective-permute-start.9 = (bf16[256,2048]{1,0:T(8,128)(2,1)}, bf16[256,2048]{1,0:T(8,128)(2,1)}, u32[]{:S(2)}, u32[]{:S(2)}) collective-permute-start(bf16[256,2048]{1,0:T(8,128)(2,1)} %bitcast.165), channel_id=1, source_target_pairs={{0,64},{64,0},{128,192},{192,128},{1,65},{65,1},{129,193},{193,129... | collective-permute-start | bytes 3145736 | tf_op jit(solution)/shard_map/ppermute | solution.py:17
  114.0 78.0 %collective-permute-start.10 = (bf16[2048,512]{1,0:T(8,128)(2,1)}, bf16[2048,512]{1,0:T(8,128)(2,1)}, u32[]{:S(2)}, u32[]{:S(2)}) collective-permute-start(bf16[2048,512]{1,0:T(8,128)(2,1)} %collective-permute-done.6), channel_id=1, source_target_pairs={{0,64},{64,0},{128,192},{192,128},{1,65},{65,1},{129,193},{193,129... | collective-permute-start | bytes 6291464 | tf_op jit(solution)/shard_map/ppermute | solution.py:17
  158.4 36.8 %collective-permute-start.11 = (bf16[256,2048]{1,0:T(8,128)(2,1)}, bf16[256,2048]{1,0:T(8,128)(2,1)}, u32[]{:S(2)}, u32[]{:S(2)}) collective-permute-start(bf16[256,2048]{1,0:T(8,128)(2,1)} %collective-permute-done.7), channel_id=1, source_target_pairs={{0,64},{64,0},{128,192},{192,128},{1,65},{65,1},{129,193},{193,129... | collective-permute-start | bytes 3145736 | tf_op jit(solution)/shard_map/ppermute | solution.py:17
  176.5 4.0 %copy-start.6 = (bf16[640,2048]{1,0:T(8,128)(2,1)S(1)}, bf16[640,2048]{1,0:T(8,128)(2,1)}, u32[]{:S(2)}) copy-start(bf16[640,2048]{1,0:T(8,128)(2,1)} %reshape.338) | copy-start | bytes 7864324
  180.6 3.2 %copy-start.11 = (bf16[1,256,2048]{2,1,0:T(8,128)(2,1)S(1)}, bf16[1,256,2048]{2,1,0:T(8,128)(2,1)}, u32[]{:S(2)}) copy-start(bf16[1,256,2048]{2,1,0:T(8,128)(2,1)} %param.17) | copy-start | bytes 3145732
  201.0 7.2 %copy-start.10 = (f32[1,256,2]{1,2,0:T(2,128)S(1)}, f32[1,256,2]{1,2,0:T(2,128)}, u32[]{:S(2)}) copy-start(f32[1,256,2]{1,2,0:T(2,128)} %param.15) | copy-start | bytes 6148
  201.0 67.6 %all-to-all-start.1 = ((bf16[64,80,256]{2,1,0:T(8,128)(2,1)}), bf16[64,80,256]{2,1,0:T(8,128)(2,1)}, u32[]{:S(2)}, u32[]{:S(2)}) async-start(bf16[64,80,256]{2,1,0:T(8,128)(2,1)} %reshape.339), calls=%async_computation.1 | async-start | bytes 5242880 | tf_op jit(solution)/shard_map/all_to_all | solution.py:111
  (2 other events, 2.5 us)
